TPU v7x, 32 devices: a whole 2x2x4 slice. The times are simulated.
32 devices in a mesh: groups: 2 (over x), dp: 16 (over z, y, core).
Axes of the slice: x: 2, y: 2, z: 4, core: 2. Of those that a mesh axis runs over, the one named last changes fastest.
Arguments:
- layer_input: bfloat16 [8192, 8192], P(('groups', 'dp')), parts along dimension 0, may hold values from -6 to 6
- grad_values: bfloat16 [8192, 1024], P(('groups', 'dp')), parts along dimension 0, may hold values from -6 to 6
- base_weight: bfloat16 [8192, 1024], P('dp'), may hold values from -0.0625 to 0.0625
- tile_ids: int32 [32], P(('groups', 'dp')), parts along dimension 0, may hold values from 0 to 511, as said below
- tile_delta: bfloat16 [32, 128, 128], P(('groups', 'dp')), parts along dimension 0, may hold values from -0.1875 to 0.1875
Outputs:
- grad_input: bfloat16 [8192, 8192], P(('groups', 'dp')), parts along dimension 0
- grad_tiles: float32 [32, 128, 128], P(('groups', 'dp')), parts along dimension 0
There are 2 independent parts, one for each index of `groups`. A program takes and returns all parts, laid end to end along the dimension named above; an argument that names none is the same for every part. Nothing has to cross between parts.
Inputs may be any that keep to these rules, and one draw needn't show every extreme that they name: `tile_ids`: the 16 tile numbers are distinct; every tile of some tile row is listed.
All inputs are finite; a program needn't handle non-finite values.
Results may differ from a plain program's by a relative error of at most 0.0034.
Values may be sent and summed in bfloat16 or wider, within the bound.
No kernel may reach another device: no remote copies, remote signals or barrier semaphores. Data moves between devices by JAX's collectives and lax.ppermute only.
A program may use at most 128 MiB of HBM per device.

v0:
```python
import math

import jax
import jax.numpy as jnp
from jax import lax
from jax.sharding import PartitionSpec as P

TILE = 128
ROW_TILES = 64
COL_TILES = 8


def delta_matrix(tile_ids, tile_delta):
    tile_rows = tile_ids // COL_TILES
    tile_cols = tile_ids % COL_TILES
    field = jnp.zeros((ROW_TILES, TILE, COL_TILES, TILE), tile_delta.dtype)
    field = field.at[tile_rows, :, tile_cols, :].set(tile_delta)
    return field.reshape(ROW_TILES * TILE, COL_TILES * TILE)


def whole_field(all_ids, tile_delta):
    all_deltas = lax.all_gather(tile_delta, "dp", axis=0, tiled=True)
    return delta_matrix(all_ids, all_deltas)


def body(layer_input, grad_values, base_weight, tile_ids, tile_delta):
    all_ids = lax.all_gather(tile_ids, "dp", axis=0, tiled=True)
    own_rows = base_weight.shape[0]
    field = whole_field(all_ids, tile_delta)
    first_row = lax.axis_index("dp") * own_rows
    own_field = lax.dynamic_slice_in_dim(field, first_row, own_rows, 0)
    merged = (base_weight.astype(jnp.float32) + own_field.astype(jnp.float32)).astype(jnp.bfloat16)
    grad_input = lax.dot_general(
        grad_values,
        lax.all_gather(merged, "dp", axis=0, tiled=True),
        (((1,), (1,)), ((), ())),
        preferred_element_type=jnp.float32,
    ).astype(jnp.bfloat16)
    tokens_here = layer_input.shape[0]
    input_panels = layer_input.reshape(tokens_here, ROW_TILES, TILE)
    grad_panels = grad_values.reshape(tokens_here, COL_TILES, TILE)
    rows_taken = jnp.take(input_panels, all_ids // COL_TILES, axis=1)
    cols_taken = jnp.take(grad_panels, all_ids % COL_TILES, axis=1)
    summed = lax.psum_scatter(
        jnp.einsum("tja,tjb->jab", rows_taken, cols_taken, preferred_element_type=jnp.float32),
        "dp",
        scatter_dimension=0,
        tiled=True,
    )
    factor = 1.0 / math.sqrt(tokens_here * lax.axis_size("dp"))
    return (grad_input, summed * factor)


def solution(mesh):
    placed = (
        P(("groups", "dp"), None),
        P(("groups", "dp"), None),
        P("dp", None),
        P(("groups", "dp")),
        P(("groups", "dp"), None, None),
    )
    return jax.shard_map(
        body,
        mesh=mesh,
        in_specs=placed,
        out_specs=(P(("groups", "dp"), None), P(("groups", "dp"), None, None)),
        check_vma=False,
    )
```

profile of v0, /device:TPU:0, one launch (start us, length us, event | category | flops | bytes accessed | tf_op | source)
XLA Modules:
  0.0 252.2 jit_solution(3247052467888750626)
XLA Ops:
  7.2 0.0 reduce-scatter.2.cloned.1.call-start
  7.9 1.2 dynamic-slice
  9.1 0.8 dynamic-update-slice
  9.9 13.8 %all-reduce = s32[16]{0:T(128)S(1)} all-reduce(s32[16]{0:T(128)S(1)} %dynamic-update-slice), channel_id=1, replica_groups=mesh['groups'=2,'dp'=16] {'dp'}, use_global_device_ids=true, to_apply=%add | all-reduce | flops 16 | bytes 128
  23.6 1.2 copy.22
  24.9 0.3 copy.23
  25.2 6.4 %copy.20 = bf16[256,8192]{0,1:T(8,128)(2,1)} copy(bf16[256,8192]{1,0:T(8,128)(2,1)} %param.5) | data formatting | bytes 8388608 | tf_op args[0]
  31.5 6.4 %copy.21 = bf16[256,64,128]{2,0,1:T(8,128)(2,1)} copy(bf16[256,64,128]{0,2,1:T(8,128)(2,1)} %bitcast.30) | data formatting | bytes 8388608 | tf_op jit(solution)/shard_map/reshape | solution.py:40
  37.9 0.7 gather_fusion.1
  38.7 2.9 %gather_fusion = bf16[16,256,128]{2,1,0:T(8,128)(2,1)S(1)} fusion(bf16[256,64,128]{2,0,1:T(8,128)(2,1)} %copy.21, s32[1024]{0:T(1024)S(1)} %get-tuple-element.17), kind=kCustom, calls=%fused_computation | custom fusion | bytes 2097216 | tf_op jit(solution)/shard_map/jit(_take)/gather | solution.py:42
  41.6 1.5 fusion.1
  43.2 0.0 all-gather.2.cloned.1.call-start
  43.3 19.4 %all_gather.10 = bf16[16,128,128]{2,1,0:T(8,128)(2,1)S(1)} all-gather(bf16[1,128,128]{2,1,0:T(8,128)(2,1)S(1)} %copy-done.2), channel_id=1, replica_groups=mesh['groups'=2,'dp'=16] {'dp'}, dimensions={0}, use_global_device_ids=true | all-gather | bytes 557056 | tf_op jit(solution)/shard_map/all_gather | solution.py:22
  62.6 6.3 %broadcast_in_dim.27 = bf16[64,128,8,128]{3,1,2,0:T(8,128)(2,1)} broadcast(bf16[]{:T(256)} %constant.62.clone.1), dimensions={} | broadcast | bytes 16777218 | tf_op jit(solution)/shard_map/broadcast_in_dim | solution.py:16
  69.0 2.7 %scatter_fusion = bf16[64,128,8,128]{3,1,2,0:T(8,128)(2,1)} fusion(bf16[64,128,8,128]{3,1,2,0:T(8,128)(2,1)} %broadcast_in_dim.27, s32[16]{0:T(128)S(1)} %fusion.10, bf16[16,128,128]{2,1,0:T(8,128)(2,1)S(1)} %all_gather.10), kind=kCustom, calls=%fused_computation.2 | custom fusion | bytes 1572992 | tf_op jit(solution)/shard_map/scatter | solution.py:17
  71.7 16.8 %copy.19 = bf16[64,128,8,128]{3,2,1,0:T(8,128)(2,1)S(1)} copy(bf16[64,128,8,128]{3,1,2,0:T(8,128)(2,1)} %scatter_fusion) | data formatting | bytes 33554432 | tf_op jit(solution)/shard_map/scatter | solution.py:17
  88.6 9.1 %copy.29 = bf16[1024,8,8,128]{3,1,2,0:T(8,128)(2,1)} copy(bf16[1024,8,8,128]{3,2,1,0:T(8,128)(2,1)S(1)} %bitcast.28) | data formatting | bytes 33554432
  97.7 2.6 %add_convert_fusion = bf16[512,1024]{1,0:T(8,128)(2,1)} fusion(bf16[512,1024]{1,0:T(8,128)(2,1)S(1)} %copy-done, bf16[8192,1024]{1,0:T(8,128)(2,1)} %bitcast.29, s32[]{:T(128)S(6)} %select_n.40), kind=kLoop, calls=%fused_computation.6 | loop fusion | flops 2097152 | bytes 3145732 | tf_op jit(solution)/shard_map/convert_element_type | solution.py:32
  100.3 0.0 all-gather.2.cloned.1.call-update
  100.3 0.0 reduce-scatter.2.cloned.1.call-done
  100.3 1.5 broadcast_multiply_fusion
  101.8 124.9 %all-gather.2.cloned.1.call-done = bf16[8192,1024]{1,0:T(8,128)(2,1)} async-done(((bf16[512,1024]{1,0:T(8,128)(2,1)}), bf16[8192,1024]{1,0:T(8,128)(2,1)}) %all-gather.2.cloned.1.call-update) | async-done | bytes 16777232 | tf_op jit(solution)/shard_map/all_gather | solution.py:35
  226.7 12.3 %fusion = bf16[256,8192]{0,1:T(8,128)(2,1)} fusion(bf16[8192,1024]{1,0:T(8,128)(2,1)} %all-gather.2.cloned.1.call-done, bf16[256,1024]{1,0:T(8,128)(2,1)S(1)} %copy-done.1), kind=kOutput, calls=%fused_computation.5 | convolution fusion | flops 4297064448 | bytes 21495808 | tf_op jit(solution)/shard_map/dot_general | solution.py:33
  239.0 6.3 %copy.25 = bf16[256,8192]{1,0:T(8,128)(2,1)} copy(bf16[256,8192]{0,1:T(8,128)(2,1)} %fusion) | data formatting | bytes 8388608
  (11 shorter events, 0.1 us)
Async XLA Ops:
  7.2 36.1 %copy-start.2 = (bf16[1,128,128]{2,1,0:T(8,128)(2,1)S(1)}, bf16[1,128,128]{2,1,0:T(8,128)(2,1)}, u32[]{:S(2)}) copy-start(bf16[1,128,128]{2,1,0:T(8,128)(2,1)} %param.9) | copy-start | bytes 98308
  7.2 93.2 %reduce-scatter.2.cloned.1.call-start = ((), (), s32[]{:S(2)}) async-start(), calls=%async_computation.2 | async-start | bytes 1114112 | tf_op jit(solution)/shard_map/reduce_scatter | solution.py:44
  43.2 183.5 %all-gather.2.cloned.1.call-start = ((), (), s32[]{:S(2)}) async-start(), calls=%async_computation.1 | async-start | bytes 17825792 | tf_op jit(solution)/shard_map/all_gather | solution.py:35
  88.5 9.1 %copy-start = (bf16[512,1024]{1,0:T(8,128)(2,1)S(1)}, bf16[512,1024]{1,0:T(8,128)(2,1)}, u32[]{:S(2)}) copy-start(bf16[512,1024]{1,0:T(8,128)(2,1)} %param.7) | copy-start | bytes 3145732
  88.6 138.2 %copy-start.1 = (bf16[256,1024]{1,0:T(8,128)(2,1)S(1)}, bf16[256,1024]{1,0:T(8,128)(2,1)}, u32[]{:S(2)}) copy-start(bf16[256,1024]{1,0:T(8,128)(2,1)} %param.6) | copy-start | bytes 1572868
Sparse Core Ops, SparseCore 0:
  43.3 55.1 reduce-scatter.1
  101.3 125.3 all-gather.1
where the time goes:
time: 253 us; the launch traced here: 252 us
  waiting for transfers between devices  125 us (49%)
  local copies, waits for them, and re-layouts  61.3 us (24%)
  blocking collectives  33.1 us (13%)
  between operations  14.8 us (6%)
  matrix products  13.8 us (5%)
  other arithmetic  4.11 us (2%)
    all_gather x1, waiting for transfers between devices, body(): lax.all_gather(merged, 'dp', axis=0, tiled=True)  125 us
    unnamed x13, local copies, waits for them, and re-layouts  25.1 us
    scatter x2, local copies, waits for them, and re-layouts, delta_matrix(): field = field.at[tile_rows, :, tile_cols, :].set(tile_delta)  19.6 us
    all_gather x1, blocking collectives, whole_field(): all_deltas = lax.all_gather(tile_delta, 'dp', axis=0, tiled=True)  19.4 us
    unnamed x1, blocking collectives  13.8 us
    dot_general x1, matrix products, body(): lax.dot_general(grad_values, lax.all_gather(merged, 'dp', axis=0, tiled=T...  12.3 us
    reshape x1, local copies, waits for them, and re-layouts, body(): input_panels = layer_input.reshape(tokens_here, ROW_TILES, TILE)  6.37 us
    broadcast_in_dim x1, local copies, waits for them, and re-layouts, delta_matrix(): field = jnp.zeros((ROW_TILES, TILE, COL_TILES, TILE), tile_delta.dtype)  6.31 us
  transfers between devices with their start and end apart: 2, of which 1 were waited for; matrix products, arithmetic and copies ran while one was open for 16% of the time, Pallas kernels for 0%

commit v1 on v0

v1 whole, which is shorter than its diff:
```python
import math

import jax
import jax.numpy as jnp
from jax import lax
from jax.experimental import pallas as pl
from jax.experimental.pallas import tpu as pltpu
from jax.sharding import PartitionSpec as P

TILE = 128
BLOCK_ROWS = 1024


def merged_matmul(tile_rows, tile_cols, grad_values, full_base, all_deltas, interpret=False):
    tokens, kv = grad_values.shape
    d_model = full_base.shape[0]
    listed = all_deltas.shape[0]
    col_tiles = kv // TILE
    tiles_per_block = BLOCK_ROWS // TILE

    def kernel(rows_ref, cols_ref, gv_ref, base_ref, delta_ref, out_ref):
        i = pl.program_id(0)

        def patch(j, carry):
            r = rows_ref[j] - i * tiles_per_block

            @pl.when((r >= 0) & (r < tiles_per_block))
            def _():
                c = cols_ref[j]
                rs = pl.ds(pl.multiple_of(r * TILE, TILE), TILE)
                for cc in range(col_tiles):

                    @pl.when(c == cc)
                    def _():
                        cs = slice(cc * TILE, (cc + 1) * TILE)
                        cur = base_ref[rs, cs].astype(jnp.float32)
                        add = delta_ref[j].astype(jnp.float32)
                        base_ref[rs, cs] = (cur + add).astype(jnp.bfloat16)

            return carry

        lax.fori_loop(0, listed, patch, 0)
        out_ref[...] = lax.dot_general(
            gv_ref[...],
            base_ref[...],
            (((1,), (1,)), ((), ())),
            preferred_element_type=jnp.float32,
        ).astype(out_ref.dtype)

    return pl.pallas_call(
        kernel,
        grid_spec=pltpu.PrefetchScalarGridSpec(
            num_scalar_prefetch=2,
            grid=(d_model // BLOCK_ROWS,),
            in_specs=[
                pl.BlockSpec((tokens, kv), lambda i, r, c: (0, 0)),
                pl.BlockSpec((BLOCK_ROWS, kv), lambda i, r, c: (i, 0)),
                pl.BlockSpec((listed, TILE, TILE), lambda i, r, c: (0, 0, 0)),
            ],
            out_specs=pl.BlockSpec((tokens, BLOCK_ROWS), lambda i, r, c: (0, i)),
        ),
        out_shape=jax.ShapeDtypeStruct((tokens, d_model), jnp.bfloat16),
        interpret=interpret,
    )(tile_rows, tile_cols, grad_values, full_base, all_deltas)


def body(layer_input, grad_values, base_weight, tile_ids, tile_delta):
    n = lax.axis_size("dp")
    tokens_here = layer_input.shape[0]
    d_model = layer_input.shape[1]
    kv = grad_values.shape[1]
    row_tiles = d_model // TILE
    col_tiles = kv // TILE

    full_base = lax.all_gather(base_weight, "dp", axis=0, tiled=True)

    all_ids = lax.all_to_all(jnp.broadcast_to(tile_ids, (n,)), "dp", 0, 0, tiled=True)
    all_deltas = lax.all_to_all(
        jnp.broadcast_to(tile_delta, (n, TILE, TILE)), "dp", 0, 0, tiled=True
    )
    tile_rows = all_ids // col_tiles
    tile_cols = all_ids % col_tiles

    input_panels = layer_input.reshape(tokens_here, row_tiles, TILE)
    grad_panels = grad_values.reshape(tokens_here, col_tiles, TILE)
    rows_taken = jnp.take(input_panels, tile_rows, axis=1)
    cols_taken = jnp.take(grad_panels, tile_cols, axis=1)
    partial = jnp.einsum(
        "tja,tjb->jab", rows_taken, cols_taken, preferred_element_type=jnp.float32
    )
    from_each = lax.all_to_all(partial, "dp", 0, 0, tiled=True)
    factor = 1.0 / math.sqrt(tokens_here * n)
    grad_tiles = jnp.sum(from_each, axis=0, keepdims=True) * factor

    grad_input = merged_matmul(tile_rows, tile_cols, grad_values, full_base, all_deltas)
    return (grad_input, grad_tiles)


def solution(mesh):
    placed = (
        P(("groups", "dp"), None),
        P(("groups", "dp"), None),
        P("dp", None),
        P(("groups", "dp")),
        P(("groups", "dp"), None, None),
    )
    return jax.shard_map(
        body,
        mesh=mesh,
        in_specs=placed,
        out_specs=(P(("groups", "dp"), None), P(("groups", "dp"), None, None)),
        check_vma=False,
    )
```

time: 253 us -> 188 us (0.74)
  waiting for transfers between devices: 125 us -> 79.9 us
  local copies, waits for them, and re-layouts: 61.3 us -> 19.7 us
  Pallas kernels: 0 us -> 14 us
  matrix products: 13.8 us -> 0.57 us
  starting transfers between devices: 0.08 us -> 12.1 us
  blocking collectives: 33.1 us -> 44.3 us
    all_gather x1, waiting for transfers between devices: 125 us -> 56.8 us  [body(): full_base = lax.all_gather(base_weight, 'dp', axis=0, tiled=True)]
    all_to_all x0 -> x1, blocking collectives: none -> 44.3 us  [body(): from_each = lax.all_to_all(partial, 'dp', 0, 0, tiled=True)]
    all_to_all x0 -> x2, waiting for transfers between devices: none -> 22.4 us  [the longest x1 22.4 us: body(): lax.all_to_all(jnp.broadcast_to(tile_delta, (n, TILE, TILE)), 'dp', 0, 0,...]
    scatter x2 -> x0, local copies, waits for them, and re-layouts: 19.6 us -> none  [delta_matrix(): field = field.at[tile_rows, :, tile_cols, :].set(tile_delta)]
    all_gather x1 -> x0, blocking collectives: 19.4 us -> none  [whole_field(): all_deltas = lax.all_gather(tile_delta, 'dp', axis=0, tiled=True)]
    unnamed x13 -> x6, local copies, waits for them, and re-layouts: 25.1 us -> 7.81 us
    pallas_call x0 -> x1, Pallas kernels: none -> 14 us  [merged_matmul(): pl.pallas_call(kernel, grid_spec=pltpu.PrefetchScalarGridSpec(num_scalar_...]
    unnamed x1 -> x0, blocking collectives: 13.8 us -> none
  transfers between devices with their start and end apart: 2 -> 3, of which waited for: 1 -> 2; matrix products, arithmetic and copies ran while one was open for 16% -> 12% of each run, Pallas kernels for 0% -> 0%
where the time goes in v1:
time: 188 us; the launch traced here: 187 us
  waiting for transfers between devices  79.9 us (43%)
  blocking collectives  44.3 us (24%)
  local copies, waits for them, and re-layouts  19.7 us (10%)
  between operations  14.7 us (8%)
  Pallas kernels  14 us (7%)
  starting transfers between devices  12.1 us (6%)
    all_gather x1, waiting for transfers between devices, body(): full_base = lax.all_gather(base_weight, 'dp', axis=0, tiled=True)  56.8 us
    all_to_all x1, blocking collectives, body(): from_each = lax.all_to_all(partial, 'dp', 0, 0, tiled=True)  44.3 us
    all_to_all x1, waiting for transfers between devices, body(): lax.all_to_all(jnp.broadcast_to(tile_delta, (n, TILE, TILE)), 'dp', 0, 0,...  22.4 us
    pallas_call x1, Pallas kernels, merged_matmul(): pl.pallas_call(kernel, grid_spec=pltpu.PrefetchScalarGridSpec(num_scalar_...  14 us
    unnamed x6, local copies, waits for them, and re-layouts  7.81 us
    all_to_all x1, starting transfers between devices, body(): lax.all_to_all(jnp.broadcast_to(tile_ids, (n,)), 'dp', 0, 0, tiled=True)  7.41 us
    reshape x1, local copies, waits for them, and re-layouts, body(): input_panels = layer_input.reshape(tokens_here, row_tiles, TILE)  6.36 us
    all_to_all x1, starting transfers between devices, body(): lax.all_to_all(jnp.broadcast_to(tile_delta, (n, TILE, TILE)), 'dp', 0, 0,...  4.67 us
  transfers between devices with their start and end apart: 3, of which 2 were waited for; matrix products, arithmetic and copies ran while one was open for 12% of the time, Pallas kernels for 0%

profile of v1, /device:TPU:0, one launch (start us, length us, event | category | flops | bytes accessed | tf_op | source)
XLA Modules:
  0.0 186.9 jit_solution(5129260228444055976)
XLA Ops:
  7.2 0.0 all-gather.2.cloned.1.call-start
  7.2 0.7 all-gather.2.cloned.1.call-update
  8.5 0.6 broadcast_in_dim.34
  9.1 7.4 %all-to-all-start = ((s32[16,1,1]{2,1,0:T(1,128)}), s32[16,1,1]{2,1,0:T(1,128)S(1)}, u32[]{:S(2)}, u32[]{:S(2)}) async-start(s32[16,1,1]{2,1,0:T(1,128)} %broadcast_in_dim.34), calls=%async_computation | async-start | bytes 16384 | tf_op jit(solution)/shard_map/all_to_all | solution.py:77
  16.6 1.2 copy.21
  17.8 0.3 copy.22
  18.1 6.5 %copy.19 = bf16[256,8192]{0,1:T(8,128)(2,1)} copy(bf16[256,8192]{1,0:T(8,128)(2,1)} %param.5) | data formatting | bytes 8388608 | tf_op args[0]
  24.6 6.4 %copy.20 = bf16[256,64,128]{2,0,1:T(8,128)(2,1)} copy(bf16[256,64,128]{0,2,1:T(8,128)(2,1)} %bitcast.34) | data formatting | bytes 8388608 | tf_op jit(solution)/shard_map/reshape | solution.py:84
  31.0 0.0 all-to-all-done
  31.0 0.4 reduce
  31.4 0.7 gather_fusion.1
  32.2 0.0 copy-start.1
  32.2 3.0 %gather_fusion = bf16[16,256,128]{2,1,0:T(8,128)(2,1)S(1)} fusion(bf16[256,64,128]{2,0,1:T(8,128)(2,1)} %copy.20, s32[1024]{0:T(1024)S(1)} %get-tuple-element.11), kind=kCustom, calls=%fused_computation | custom fusion | bytes 2097216 | tf_op jit(solution)/shard_map/jit(_take)/gather | solution.py:86
  35.2 0.6 compare_and_fusion
  35.8 0.6 fusion
  36.3 44.3 %all_to_all.22 = f32[16,128,128]{2,1,0:T(8,128)S(1)} all-to-all(f32[16,128,128]{2,1,0:T(8,128)S(1)} %fusion), channel_id=1, replica_groups=mesh['groups'=2,'dp'=16] {'dp'}, dimensions={0} | all-to-all | bytes 2097152 | tf_op jit(solution)/shard_map/all_to_all | solution.py:91
  80.7 0.9 broadcast_in_dim.36
  81.6 4.7 %all-to-all-start.1 = ((bf16[16,128,128]{2,1,0:T(8,128)(2,1)}), bf16[16,128,128]{2,1,0:T(8,128)(2,1)S(1)}, u32[]{:S(2)}, u32[]{:S(2)}) async-start(bf16[16,128,128]{2,1,0:T(8,128)(2,1)} %broadcast_in_dim.36), calls=%async_computation.1 | async-start | bytes 1048576 | tf_op jit(solution)/shard_map/all_to_all | solution.py:78
  86.2 0.1 reduce_sum.9
  86.3 0.6 multiply_bitcast_fusion
  86.9 22.4 %all-to-all-done.1.delta_ref = bf16[16,128,128]{2,1,0:T(8,128)(2,1)S(1)} async-done(((bf16[16,128,128]{2,1,0:T(8,128)(2,1)}), bf16[16,128,128]{2,1,0:T(8,128)(2,1)S(1)}, u32[]{:S(2)}, u32[]{:S(2)}) %all-to-all-start.1) | async-done | bytes 524320 | tf_op jit(solution)/shard_map/all_to_all | solution.py:78
  109.3 56.8 %all-gather.2.cloned.1.call-done.base_ref = bf16[8192,1024]{1,0:T(8,128)(2,1)} async-done(((bf16[512,1024]{1,0:T(8,128)(2,1)}), bf16[8192,1024]{1,0:T(8,128)(2,1)}) %all-gather.2.cloned.1.call-update) | async-done | bytes 16777232 | tf_op jit(solution)/shard_map/all_gather | solution.py:75
  166.1 0.0 copy-done
  166.1 14.0 %shard_map.68 = bf16[256,8192]{1,0:T(8,128)(2,1)} custom-call(s32[16]{0:T(128)} %get-tuple-element.9.rows_ref, s32[16]{0:T(128)} %get-tuple-element.5.cols_ref, bf16[256,1024]{1,0:T(8,128)(2,1)} %gv_ref.1, bf16[8192,1024]{1,0:T(8,128)(2,1)} %all-gather.2.cloned.1.call-done.base_ref, bf16[16,128,128]{2,1,0:T(8,128)(2,1)} %copy-done), custom_call_target="tpu_custom_call" | custom-call | tf_op jit(solution)/shard_map/pallas_call | solution.py:50
  (4 shorter events, 0.0 us)
Async XLA Ops:
  7.2 159.0 %all-gather.2.cloned.1.call-start = ((), (), s32[]{:S(2)}) async-start(), calls=%async_computation.3 | async-start | bytes 17825792 | tf_op jit(solution)/shard_map/all_gather | solution.py:75
  9.1 21.9 %all-to-all-start = ((s32[16,1,1]{2,1,0:T(1,128)}), s32[16,1,1]{2,1,0:T(1,128)S(1)}, u32[]{:S(2)}, u32[]{:S(2)}) async-start(s32[16,1,1]{2,1,0:T(1,128)} %broadcast_in_dim.34), calls=%async_computation | async-start | bytes 16384 | tf_op jit(solution)/shard_map/all_to_all | solution.py:77
  32.2 48.5 %copy-start.1 = (bf16[1,128,128]{2,1,0:T(8,128)(2,1)S(1)}, bf16[1,128,128]{2,1,0:T(8,128)(2,1)}, u32[]{:S(2)}) copy-start(bf16[1,128,128]{2,1,0:T(8,128)(2,1)} %param.9) | copy-start | bytes 98308
  81.6 27.7 %all-to-all-start.1 = ((bf16[16,128,128]{2,1,0:T(8,128)(2,1)}), bf16[16,128,128]{2,1,0:T(8,128)(2,1)S(1)}, u32[]{:S(2)}, u32[]{:S(2)}) async-start(bf16[16,128,128]{2,1,0:T(8,128)(2,1)} %broadcast_in_dim.36), calls=%async_computation.1 | async-start | bytes 1048576 | tf_op jit(solution)/shard_map/all_to_all | solution.py:78
  109.3 56.8 %copy-start = (bf16[16,128,128]{2,1,0:T(8,128)(2,1)}, bf16[16,128,128]{2,1,0:T(8,128)(2,1)S(1)}, u32[]{:S(2)}) copy-start(bf16[16,128,128]{2,1,0:T(8,128)(2,1)S(1)} %all-to-all-done.1.delta_ref) | copy-start | bytes 1572868
Sparse Core Ops, SparseCore 0:
  10.1 155.9 all-gather.1

commit v2 on v1

v2 whole, which is shorter than its diff:
```python
import math

import jax
import jax.numpy as jnp
from jax import lax
from jax.experimental import pallas as pl
from jax.experimental.pallas import tpu as pltpu
from jax.sharding import Mesh
from jax.sharding import PartitionSpec as P

TILE = 128
BLOCK_ROWS = 1024
DP = ("chips", "core")


def merged_matmul(tile_rows, tile_cols, grad_values, gathered, shard, all_deltas, interpret=False):
    tokens, kv = grad_values.shape
    n = gathered.shape[0]
    d_model = n * shard
    listed = all_deltas.shape[0]
    col_tiles = kv // TILE
    block_rows = max(BLOCK_ROWS, shard)
    per_block = block_rows // shard
    tiles_per_block = block_rows // TILE
    piece = min(shard, TILE)

    def kernel(rows_ref, cols_ref, gv_ref, base_ref, delta_ref, out_ref):
        i = pl.program_id(0)

        def patch(j, carry):
            r = rows_ref[j] - i * tiles_per_block

            @pl.when((r >= 0) & (r < tiles_per_block))
            def _():
                c = cols_ref[j]
                for q in range(TILE // piece):
                    at = r * TILE + q * piece
                    si = at // shard
                    rs = pl.ds(pl.multiple_of(at % shard, piece), piece)
                    for cc in range(col_tiles):

                        @pl.when(c == cc)
                        def _():
                            cs = slice(cc * TILE, (cc + 1) * TILE)
                            cur = base_ref[si, rs, cs].astype(jnp.float32)
                            add = delta_ref[j, q * piece:(q + 1) * piece, :].astype(jnp.float32)
                            base_ref[si, rs, cs] = (cur + add).astype(jnp.bfloat16)

            return carry

        lax.fori_loop(0, listed, patch, 0)
        merged = base_ref[...].reshape(block_rows, kv)
        out_ref[...] = lax.dot_general(
            gv_ref[...],
            merged,
            (((1,), (1,)), ((), ())),
            preferred_element_type=jnp.float32,
        ).astype(out_ref.dtype)

    return pl.pallas_call(
        kernel,
        grid_spec=pltpu.PrefetchScalarGridSpec(
            num_scalar_prefetch=2,
            grid=(d_model // block_rows,),
            in_specs=[
                pl.BlockSpec((tokens, kv), lambda i, r, c: (0, 0)),
                pl.BlockSpec((per_block, shard, kv), lambda i, r, c: (i, 0, 0)),
                pl.BlockSpec((listed, TILE, TILE), lambda i, r, c: (0, 0, 0)),
            ],
            out_specs=pl.BlockSpec((tokens, block_rows), lambda i, r, c: (0, i)),
        ),
        out_shape=jax.ShapeDtypeStruct((tokens, d_model), jnp.bfloat16),
        interpret=interpret,
    )(tile_rows, tile_cols, grad_values, gathered, all_deltas)


def body(layer_input, grad_values, base_weight, tile_ids, tile_delta):
    chips = lax.axis_size("chips")
    n = 2 * chips
    tokens_here = layer_input.shape[0]
    d_model = layer_input.shape[1]
    kv = grad_values.shape[1]
    shard = base_weight.shape[0]
    row_tiles = d_model // TILE
    col_tiles = kv // TILE

    packed = jnp.concatenate([base_weight, tile_delta.reshape(-1, kv)], axis=0)
    gathered = lax.all_gather(packed, DP, axis=0, tiled=False)

    all_ids = lax.all_to_all(jnp.broadcast_to(tile_ids, (n,)), DP, 0, 0, tiled=True)
    tile_rows = all_ids // col_tiles
    tile_cols = all_ids % col_tiles

    input_panels = layer_input.reshape(tokens_here, row_tiles, TILE)
    grad_panels = grad_values.reshape(tokens_here, col_tiles, TILE)
    rows_taken = jnp.take(input_panels, tile_rows, axis=1)
    cols_taken = jnp.take(grad_panels, tile_cols, axis=1)
    partial = jnp.einsum(
        "tja,tjb->jab", rows_taken, cols_taken, preferred_element_type=jnp.float32
    ).reshape(chips, 2, TILE, TILE)
    core = lax.axis_index("core")
    mine = lax.dynamic_index_in_dim(partial, core, axis=1, keepdims=False)
    other = lax.dynamic_index_in_dim(partial, 1 - core, axis=1, keepdims=False)
    chip_sum = mine + lax.ppermute(other, "core", [(0, 1), (1, 0)])
    from_chips = lax.all_to_all(chip_sum, "chips", 0, 0, tiled=True)
    factor = 1.0 / math.sqrt(tokens_here * n)
    grad_tiles = jnp.sum(from_chips, axis=0, keepdims=True) * factor

    all_deltas = gathered[:, shard:, :].reshape(n, TILE, TILE)
    grad_input = merged_matmul(
        tile_rows, tile_cols, grad_values, gathered, shard, all_deltas
    )
    return (grad_input, grad_tiles)


def solution(mesh):
    groups, dp = mesh.devices.shape
    split = Mesh(mesh.devices.reshape(groups, dp // 2, 2), ("groups",) + DP)
    tokens = ("groups",) + DP
    placed = (
        P(tokens, None),
        P(tokens, None),
        P(DP, None),
        P(tokens),
        P(tokens, None, None),
    )
    return jax.shard_map(
        body,
        mesh=split,
        in_specs=placed,
        out_specs=(P(tokens, None), P(tokens, None, None)),
        check_vma=False,
    )
```

time: 188 us -> 139 us (0.74)
  waiting for transfers between devices: 79.9 us -> 45.2 us
  blocking collectives: 44.3 us -> 27.1 us
  starting transfers between devices: 12.1 us -> 7.89 us
  other arithmetic: 1.68 us -> 5.08 us
  local copies, waits for them, and re-layouts: 19.7 us -> 21.7 us
    all_to_all x2 -> x1, waiting for transfers between devices: 22.4 us -> 0.01 us  [body(): lax.all_to_all(jnp.broadcast_to(tile_ids, (n,)), DP, 0, 0, tiled=True)]
    all_to_all x1, blocking collectives: 44.3 us -> 27.1 us  [body(): from_chips = lax.all_to_all(chip_sum, 'chips', 0, 0, tiled=True)]
    all_gather x1, waiting for transfers between devices: 56.8 us -> 43.2 us  [body(): gathered = lax.all_gather(packed, DP, axis=0, tiled=False)]
    all_to_all x2 -> x1, starting transfers between devices: 12.1 us -> 7.41 us  [body(): lax.all_to_all(jnp.broadcast_to(tile_ids, (n,)), DP, 0, 0, tiled=True)]
    concatenate x0 -> x1, other arithmetic: none -> 2.33 us  [body(): packed = jnp.concatenate([base_weight, tile_delta.reshape(-1, kv)], axis=0)]
    ppermute x0 -> x1, waiting for transfers between devices: none -> 1.92 us  [body(): chip_sum = mine + lax.ppermute(other, 'core', [(0, 1), (1, 0)])]
  transfers between devices with their start and end apart: 3 -> 3, of which waited for: 2 -> 2; matrix products, arithmetic and copies ran while one was open for 12% -> 15% of each run, Pallas kernels for 0% -> 0%
where the time goes in v2:
time: 139 us; the launch traced here: 136 us
  waiting for transfers between devices  45.2 us (33%)
  blocking collectives  27.1 us (19%)
  local copies, waits for them, and re-layouts  21.7 us (16%)
  between operations  14.8 us (11%)
  Pallas kernels  13.9 us (10%)
  starting transfers between devices  7.89 us (6%)
  other arithmetic  5.08 us (4%)
    all_gather x1, waiting for transfers between devices, body(): gathered = lax.all_gather(packed, DP, axis=0, tiled=False)  43.2 us
    all_to_all x1, blocking collectives, body(): from_chips = lax.all_to_all(chip_sum, 'chips', 0, 0, tiled=True)  27.1 us
    pallas_call x1, Pallas kernels, merged_matmul(): pl.pallas_call(kernel, grid_spec=pltpu.PrefetchScalarGridSpec(num_scalar_...  13.9 us
    unnamed x6, local copies, waits for them, and re-layouts  7.62 us
    all_to_all x1, starting transfers between devices, body(): lax.all_to_all(jnp.broadcast_to(tile_ids, (n,)), DP, 0, 0, tiled=True)  7.41 us
    reshape x1, local copies, waits for them, and re-layouts, body(): input_panels = layer_input.reshape(tokens_here, row_tiles, TILE)  6.39 us
    gather x1, local copies, waits for them, and re-layouts, body(): rows_taken = jnp.take(input_panels, tile_rows, axis=1)  3.07 us
  transfers between devices with their start and end apart: 3, of which 2 were waited for; matrix products, arithmetic and copies ran while one was open for 15% of the time, Pallas kernels for 0%

profile of v2, /device:TPU:0, one launch (start us, length us, event | category | flops | bytes accessed | tf_op | source)
XLA Modules:
  0.0 136.2 jit_solution(10144600756217605137)
XLA Ops:
  7.2 0.0 all-gather.3.cloned.1.call-start
  7.2 0.8 reshape.163
  8.0 2.3 %pad_maximum_fusion = bf16[528,1024]{1,0:T(8,128)(2,1)} fusion(bf16[16,1024]{1,0:T(8,128)(2,1)S(1)} %reshape.163, bf16[512,1024]{1,0:T(8,128)(2,1)} %param.7), kind=kLoop, calls=%fused_computation.2 | loop fusion | flops 2162688 | bytes 2162688 | tf_op jit(solution)/shard_map/concatenate | solution.py:87
  11.0 0.6 broadcast_in_dim.27
  11.7 7.4 %all-to-all-start = ((s32[16,1,1]{2,1,0:T(1,128)}), s32[16,1,1]{2,1,0:T(1,128)S(1)}, u32[]{:S(2)}, u32[]{:S(2)}) async-start(s32[16,1,1]{2,1,0:T(1,128)} %broadcast_in_dim.27), calls=%async_computation | async-start | bytes 16384 | tf_op jit(solution)/shard_map/all_to_all | solution.py:90
  19.1 0.2 copy.21
  19.3 0.3 copy.22
  19.6 6.4 %copy.19 = bf16[256,8192]{0,1:T(8,128)(2,1)} copy(bf16[256,8192]{1,0:T(8,128)(2,1)} %param.5) | data formatting | bytes 8388608 | tf_op args[0]
  26.0 6.4 %copy.20 = bf16[256,64,128]{2,0,1:T(8,128)(2,1)} copy(bf16[256,64,128]{0,2,1:T(8,128)(2,1)} %bitcast.41) | data formatting | bytes 8388608 | tf_op jit(solution)/shard_map/reshape | solution.py:94
  32.4 0.4 reduce
  32.8 0.7 gather_fusion.1
  33.6 3.1 %gather_fusion = bf16[16,256,128]{2,1,0:T(8,128)(2,1)S(1)} fusion(bf16[256,64,128]{2,0,1:T(8,128)(2,1)} %copy.20, s32[1024]{0:T(1024)S(1)} %get-tuple-element.11), kind=kCustom, calls=%fused_computation | custom fusion | bytes 2097216 | tf_op jit(solution)/shard_map/jit(_take)/gather | solution.py:96
  36.7 0.6 compare_and_fusion
  37.2 0.6 fusion
  37.8 1.0 copy-done.1
  38.8 0.4 collective-permute-start
  39.3 1.9 %collective-permute-done = f32[8,128,128]{2,1,0:T(8,128)S(1)} collective-permute-done((f32[8,128,128]{2,1,0:T(8,128)S(1)}, f32[8,128,128]{2,1,0:T(8,128)S(1)}, u32[]{:S(2)}, u32[]{:S(2)}) %collective-permute-start) | collective-permute-done | bytes 524320 | tf_op jit(solution)/shard_map/ppermute | solution.py:104
  41.2 1.1 bitcast_add_fusion
  42.3 27.1 %all_to_all.17 = f32[8,128,128]{2,1,0:T(8,128)S(1)} all-to-all(f32[8,128,128]{2,1,0:T(8,128)S(1)} %bitcast_add_fusion), channel_id=1, replica_groups=mesh['groups'=2,'chips'=8,'core'=2] {'chips'}, dimensions={0} | all-to-all | bytes 1048576 | tf_op jit(solution)/shard_map/all_to_all | solution.py:105
  69.5 0.6 multiply_bitcast_fusion
  70.1 43.2 %all-gather.3.cloned.1.call-done = bf16[8448,1024]{1,0:T(8,128)(2,1)} async-done(((bf16[528,1024]{1,0:T(8,128)(2,1)}), bf16[8448,1024]{1,0:T(8,128)(2,1)}) %all-gather.3.cloned.1.call-update) | async-done | bytes 17301520 | tf_op jit(solution)/shard_map/all_gather | solution.py:88
  113.3 1.1 slice.8
  114.4 1.0 reshape.164.delta_ref
  115.4 13.9 %shard_map.68 = bf16[256,8192]{1,0:T(8,128)(2,1)} custom-call(s32[16]{0:T(128)} %get-tuple-element.9.rows_ref, s32[16]{0:T(128)} %get-tuple-element.5.cols_ref, bf16[256,1024]{1,0:T(8,128)(2,1)} %gv_ref.1, bf16[16,528,1024]{2,1,0:T(8,128)(2,1)} %bitcast.40, bf16[16,128,128]{2,1,0:T(8,128)(2,1)} %reshape.164.delta_ref), custom_call_target="tpu_custom_call" | custom-call | tf_op jit(solution)/shard_map/pallas_call | solution.py:60
  (9 shorter events, 0.1 us)
Async XLA Ops:
  7.2 11.9 %copy-start = (bf16[256,1024]{1,0:T(8,128)(2,1)S(1)}, bf16[256,1024]{1,0:T(8,128)(2,1)}, u32[]{:S(2)}) copy-start(bf16[256,1024]{1,0:T(8,128)(2,1)} %gv_ref.1) | copy-start | bytes 1572868
  7.2 106.1 %all-gather.3.cloned.1.call-start = ((), (), s32[]{:S(2)}) async-start(), calls=%async_computation.2 | async-start | bytes 18382848 | tf_op jit(solution)/shard_map/all_gather | solution.py:88
  11.7 20.8 %all-to-all-start = ((s32[16,1,1]{2,1,0:T(1,128)}), s32[16,1,1]{2,1,0:T(1,128)S(1)}, u32[]{:S(2)}, u32[]{:S(2)}) async-start(s32[16,1,1]{2,1,0:T(1,128)} %broadcast_in_dim.27), calls=%async_computation | async-start | bytes 16384 | tf_op jit(solution)/shard_map/all_to_all | solution.py:90
  37.8 1.0 copy-start.1
  38.8 2.4 %collective-permute-start = (f32[8,128,128]{2,1,0:T(8,128)S(1)}, f32[8,128,128]{2,1,0:T(8,128)S(1)}, u32[]{:S(2)}, u32[]{:S(2)}) collective-permute-start(f32[8,128,128]{2,1,0:T(8,128)S(1)} %dynamic-slice_bitcast_fusion), channel_id=1, source_target_pairs={{0,1},{1,0},{2,3},{3,2},{4,5},{5,4},{6,7},{7,6},{8,9},{9,8},{10,11... | collective-permute-start | bytes 1572872 | tf_op jit(solution)/shard_map/ppermute | solution.py:104
Sparse Core Ops, SparseCore 0:
  10.5 102.7 all-gather.2

commit v3 on v2

--- a/solution.py
+++ b/solution.py
@@ -9,20 +9,19 @@
 from jax.sharding import PartitionSpec as P
 
 TILE = 128
-BLOCK_ROWS = 1024
+BLOCK_ROWS = 4096
 DP = ("chips", "core")
 
 
-def merged_matmul(tile_rows, tile_cols, grad_values, gathered, shard, all_deltas, interpret=False):
+def merged_matmul(tile_rows, tile_cols, grad_values, gathered, shard, interpret=False):
     tokens, kv = grad_values.shape
-    n = gathered.shape[0]
+    n, packed_rows, _ = gathered.shape
+    sub = packed_rows - shard
     d_model = n * shard
-    listed = all_deltas.shape[0]
     col_tiles = kv // TILE
-    block_rows = max(BLOCK_ROWS, shard)
+    block_rows = max(min(BLOCK_ROWS, d_model), shard)
     per_block = block_rows // shard
     tiles_per_block = block_rows // TILE
-    piece = min(shard, TILE)
 
     def kernel(rows_ref, cols_ref, gv_ref, base_ref, delta_ref, out_ref):
         i = pl.program_id(0)
@@ -33,22 +32,22 @@
             @pl.when((r >= 0) & (r < tiles_per_block))
             def _():
                 c = cols_ref[j]
-                for q in range(TILE // piece):
-                    at = r * TILE + q * piece
+                for a in range(col_tiles):
+                    at = r * TILE + a * sub
                     si = at // shard
-                    rs = pl.ds(pl.multiple_of(at % shard, piece), piece)
+                    rs = pl.ds(pl.multiple_of(at % shard, sub), sub)
+                    add = delta_ref[j, :, a * TILE:(a + 1) * TILE].astype(jnp.float32)
                     for cc in range(col_tiles):
 
                         @pl.when(c == cc)
                         def _():
                             cs = slice(cc * TILE, (cc + 1) * TILE)
                             cur = base_ref[si, rs, cs].astype(jnp.float32)
-                            add = delta_ref[j, q * piece:(q + 1) * piece, :].astype(jnp.float32)
                             base_ref[si, rs, cs] = (cur + add).astype(jnp.bfloat16)
 
             return carry
 
-        lax.fori_loop(0, listed, patch, 0)
+        lax.fori_loop(0, n, patch, 0)
         merged = base_ref[...].reshape(block_rows, kv)
         out_ref[...] = lax.dot_general(
             gv_ref[...],
@@ -65,13 +64,13 @@
             in_specs=[
                 pl.BlockSpec((tokens, kv), lambda i, r, c: (0, 0)),
                 pl.BlockSpec((per_block, shard, kv), lambda i, r, c: (i, 0, 0)),
-                pl.BlockSpec((listed, TILE, TILE), lambda i, r, c: (0, 0, 0)),
+                pl.BlockSpec((n, sub, kv), lambda i, r, c: (0, shard // sub, 0)),
             ],
             out_specs=pl.BlockSpec((tokens, block_rows), lambda i, r, c: (0, i)),
         ),
         out_shape=jax.ShapeDtypeStruct((tokens, d_model), jnp.bfloat16),
         interpret=interpret,
-    )(tile_rows, tile_cols, grad_values, gathered, all_deltas)
+    )(tile_rows, tile_cols, grad_values, gathered, gathered)
 
 
 def body(layer_input, grad_values, base_weight, tile_ids, tile_delta):
@@ -84,7 +83,9 @@
     row_tiles = d_model // TILE
     col_tiles = kv // TILE
 
-    packed = jnp.concatenate([base_weight, tile_delta.reshape(-1, kv)], axis=0)
+    sub = TILE * TILE // kv
+    delta_rows = tile_delta.reshape(col_tiles, sub, TILE).transpose(1, 0, 2).reshape(sub, kv)
+    packed = jnp.concatenate([base_weight, delta_rows], axis=0)
     gathered = lax.all_gather(packed, DP, axis=0, tiled=False)
 
     all_ids = lax.all_to_all(jnp.broadcast_to(tile_ids, (n,)), DP, 0, 0, tiled=True)
@@ -106,10 +107,7 @@
     factor = 1.0 / math.sqrt(tokens_here * n)
     grad_tiles = jnp.sum(from_chips, axis=0, keepdims=True) * factor
 
-    all_deltas = gathered[:, shard:, :].reshape(n, TILE, TILE)
-    grad_input = merged_matmul(
-        tile_rows, tile_cols, grad_values, gathered, shard, all_deltas
-    )
+    grad_input = merged_matmul(tile_rows, tile_cols, grad_values, gathered, shard)
     return (grad_input, grad_tiles)
 
 

time: 139 us -> 138 us (level)
  local copies, waits for them, and re-layouts: 21.7 us -> 19.5 us
  Pallas kernels: 13.9 us -> 16 us
    pallas_call x1, Pallas kernels: 13.9 us -> 16 us  [merged_matmul(): pl.pallas_call(kernel, grid_spec=pltpu.PrefetchScalarGridSpec(num_scalar_...]
  transfers between devices with their start and end apart: 3 -> 3, of which waited for: 2 -> 2; matrix products, arithmetic and copies ran while one was open for 15% -> 16% of each run, Pallas kernels for 0% -> 0%
where the time goes in v3:
time: 138 us; the launch traced here: 136 us
  waiting for transfers between devices  45.1 us (33%)
  blocking collectives  27.2 us (20%)
  local copies, waits for them, and re-layouts  19.5 us (14%)
  Pallas kernels  16 us (12%)
  between operations  14.8 us (11%)
  starting transfers between devices  7.89 us (6%)
  other arithmetic  5.09 us (4%)
    all_gather x1, waiting for transfers between devices, body(): gathered = lax.all_gather(packed, DP, axis=0, tiled=False)  43.2 us
    all_to_all x1, blocking collectives, body(): from_chips = lax.all_to_all(chip_sum, 'chips', 0, 0, tiled=True)  27.2 us
    pallas_call x1, Pallas kernels, merged_matmul(): pl.pallas_call(kernel, grid_spec=pltpu.PrefetchScalarGridSpec(num_scalar_...  16 us
    unnamed x6, local copies, waits for them, and re-layouts  7.62 us
    all_to_all x1, starting transfers between devices, body(): lax.all_to_all(jnp.broadcast_to(tile_ids, (n,)), DP, 0, 0, tiled=True)  7.41 us
    reshape x1, local copies, waits for them, and re-layouts, body(): input_panels = layer_input.reshape(tokens_here, row_tiles, TILE)  6.39 us
    gather x1, local copies, waits for them, and re-layouts, body(): rows_taken = jnp.take(input_panels, tile_rows, axis=1)  3.07 us
  transfers between devices with their start and end apart: 3, of which 2 were waited for; matrix products, arithmetic and copies ran while one was open for 16% of the time, Pallas kernels for 0%

profile of v3, /device:TPU:0, one launch (start us, length us, event | category | flops | bytes accessed | tf_op | source)
XLA Modules:
  0.0 136.1 jit_solution(13318568110329770312)
XLA Ops:
  7.2 0.0 copy-start
  7.2 0.0 all-gather.3.cloned.1.call-start
  7.2 0.8 copy.32
  8.0 2.3 %pad_maximum_fusion = bf16[528,1024]{1,0:T(8,128)(2,1)} fusion(bf16[16,1024]{1,0:T(8,128)(2,1)S(1)} %bitcast.52, bf16[512,1024]{1,0:T(8,128)(2,1)} %param.7), kind=kLoop, calls=%fused_computation.2 | loop fusion | flops 2162688 | bytes 2162688 | tf_op jit(solution)/shard_map/concatenate | solution.py:88
  10.4 0.0 all-gather.3.cloned.1.call-update
  11.0 0.6 broadcast_in_dim.27
  11.6 7.4 %all-to-all-start = ((s32[16,1,1]{2,1,0:T(1,128)}), s32[16,1,1]{2,1,0:T(1,128)S(1)}, u32[]{:S(2)}, u32[]{:S(2)}) async-start(s32[16,1,1]{2,1,0:T(1,128)} %broadcast_in_dim.27), calls=%async_computation | async-start | bytes 16384 | tf_op jit(solution)/shard_map/all_to_all | solution.py:91
  19.1 0.2 copy.26
  19.3 0.3 copy.27
  19.6 6.4 %copy.24 = bf16[256,8192]{0,1:T(8,128)(2,1)} copy(bf16[256,8192]{1,0:T(8,128)(2,1)} %param.5) | data formatting | bytes 8388608 | tf_op args[0]
  26.0 6.4 %copy.25 = bf16[256,64,128]{2,0,1:T(8,128)(2,1)} copy(bf16[256,64,128]{0,2,1:T(8,128)(2,1)} %bitcast.48) | data formatting | bytes 8388608 | tf_op jit(solution)/shard_map/reshape | solution.py:95
  32.4 0.4 reduce
  32.8 0.7 gather_fusion.1
  33.6 3.1 %gather_fusion = bf16[16,256,128]{2,1,0:T(8,128)(2,1)S(1)} fusion(bf16[256,64,128]{2,0,1:T(8,128)(2,1)} %copy.25, s32[1024]{0:T(1024)S(1)} %get-tuple-element.11), kind=kCustom, calls=%fused_computation | custom fusion | bytes 2097216 | tf_op jit(solution)/shard_map/jit(_take)/gather | solution.py:97
  36.6 0.6 compare_and_fusion
  37.2 0.6 fusion
  37.8 1.0 copy-done.1
  38.8 0.4 collective-permute-start
  39.3 1.9 %collective-permute-done = f32[8,128,128]{2,1,0:T(8,128)S(1)} collective-permute-done((f32[8,128,128]{2,1,0:T(8,128)S(1)}, f32[8,128,128]{2,1,0:T(8,128)S(1)}, u32[]{:S(2)}, u32[]{:S(2)}) %collective-permute-start) | collective-permute-done | bytes 524320 | tf_op jit(solution)/shard_map/ppermute | solution.py:105
  41.2 1.1 bitcast_add_fusion
  42.3 27.2 %all_to_all.17 = f32[8,128,128]{2,1,0:T(8,128)S(1)} all-to-all(f32[8,128,128]{2,1,0:T(8,128)S(1)} %bitcast_add_fusion), channel_id=1, replica_groups=mesh['groups'=2,'chips'=8,'core'=2] {'chips'}, dimensions={0} | all-to-all | bytes 1048576 | tf_op jit(solution)/shard_map/all_to_all | solution.py:106
  69.5 0.6 multiply_bitcast_fusion
  70.1 43.2 %all-gather.3.cloned.1.call-done = bf16[8448,1024]{1,0:T(8,128)(2,1)} async-done(((bf16[528,1024]{1,0:T(8,128)(2,1)}), bf16[8448,1024]{1,0:T(8,128)(2,1)}) %all-gather.3.cloned.1.call-update) | async-done | bytes 17301520 | tf_op jit(solution)/shard_map/all_gather | solution.py:89
  113.3 16.0 %shard_map.68 = bf16[256,8192]{1,0:T(8,128)(2,1)} custom-call(s32[16]{0:T(128)} %get-tuple-element.9.rows_ref, s32[16]{0:T(128)} %get-tuple-element.5.cols_ref, bf16[256,1024]{1,0:T(8,128)(2,1)} %gv_ref.1, bf16[16,528,1024]{2,1,0:T(8,128)(2,1)} %bitcast.46, bf16[16,528,1024]{2,1,0:T(8,128)(2,1)} %bitcast.47), custom_call_target="tpu_custom_call" | custom-call | tf_op jit(solution)/shard_map/pallas_call | solution.py:59
  (7 shorter events, 0.1 us)
Async XLA Ops:
  7.2 11.9 %copy-start = (bf16[256,1024]{1,0:T(8,128)(2,1)S(1)}, bf16[256,1024]{1,0:T(8,128)(2,1)}, u32[]{:S(2)}) copy-start(bf16[256,1024]{1,0:T(8,128)(2,1)} %gv_ref.1) | copy-start | bytes 1572868
  7.2 106.1 %all-gather.3.cloned.1.call-start = ((), (), s32[]{:S(2)}) async-start(), calls=%async_computation.2 | async-start | bytes 18382848 | tf_op jit(solution)/shard_map/all_gather | solution.py:89
  11.6 20.8 %all-to-all-start = ((s32[16,1,1]{2,1,0:T(1,128)}), s32[16,1,1]{2,1,0:T(1,128)S(1)}, u32[]{:S(2)}, u32[]{:S(2)}) async-start(s32[16,1,1]{2,1,0:T(1,128)} %broadcast_in_dim.27), calls=%async_computation | async-start | bytes 16384 | tf_op jit(solution)/shard_map/all_to_all | solution.py:91
  37.8 1.0 copy-start.1
  38.8 2.3 %collective-permute-start = (f32[8,128,128]{2,1,0:T(8,128)S(1)}, f32[8,128,128]{2,1,0:T(8,128)S(1)}, u32[]{:S(2)}, u32[]{:S(2)}) collective-permute-start(f32[8,128,128]{2,1,0:T(8,128)S(1)} %dynamic-slice_bitcast_fusion), channel_id=1, source_target_pairs={{0,1},{1,0},{2,3},{3,2},{4,5},{5,4},{6,7},{7,6},{8,9},{9,8},{10,11... | collective-permute-start | bytes 1572872 | tf_op jit(solution)/shard_map/ppermute | solution.py:105
Sparse Core Ops, SparseCore 0:
  10.5 102.7 all-gather.2

commit v4 on v3

--- a/solution.py
+++ b/solution.py
@@ -13,17 +13,19 @@
 DP = ("chips", "core")
 
 
-def merged_matmul(tile_rows, tile_cols, grad_values, gathered, shard, interpret=False):
+def merged_matmul(tile_rows, tile_cols, own_group, grad_values, gathered, interpret=False):
     tokens, kv = grad_values.shape
-    n, packed_rows, _ = gathered.shape
-    sub = packed_rows - shard
+    halves, n, packed_rows, _ = gathered.shape
+    sub = TILE * TILE // kv
+    half = packed_rows - sub
+    shard = halves * half
     d_model = n * shard
     col_tiles = kv // TILE
     block_rows = max(min(BLOCK_ROWS, d_model), shard)
     per_block = block_rows // shard
     tiles_per_block = block_rows // TILE
 
-    def kernel(rows_ref, cols_ref, gv_ref, base_ref, delta_ref, out_ref):
+    def kernel(rows_ref, cols_ref, group_ref, gv_ref, base_ref, delta_ref, out_ref):
         i = pl.program_id(0)
 
         def patch(j, carry):
@@ -35,42 +37,46 @@
                 for a in range(col_tiles):
                     at = r * TILE + a * sub
                     si = at // shard
-                    rs = pl.ds(pl.multiple_of(at % shard, sub), sub)
-                    add = delta_ref[j, :, a * TILE:(a + 1) * TILE].astype(jnp.float32)
+                    gi = (at % shard) // half
+                    rs = pl.ds(pl.multiple_of(at % half, sub), sub)
+                    add = delta_ref[0, j, :, a * TILE:(a + 1) * TILE].astype(jnp.float32)
                     for cc in range(col_tiles):
 
                         @pl.when(c == cc)
                         def _():
                             cs = slice(cc * TILE, (cc + 1) * TILE)
-                            cur = base_ref[si, rs, cs].astype(jnp.float32)
-                            base_ref[si, rs, cs] = (cur + add).astype(jnp.bfloat16)
+                            cur = base_ref[gi, si, rs, cs].astype(jnp.float32)
+                            base_ref[gi, si, rs, cs] = (cur + add).astype(jnp.bfloat16)
 
             return carry
 
         lax.fori_loop(0, n, patch, 0)
-        merged = base_ref[...].reshape(block_rows, kv)
-        out_ref[...] = lax.dot_general(
-            gv_ref[...],
-            merged,
-            (((1,), (1,)), ((), ())),
-            preferred_element_type=jnp.float32,
-        ).astype(out_ref.dtype)
+        for gi in range(halves):
+            part = lax.dot_general(
+                gv_ref[...],
+                base_ref[gi].reshape(per_block * half, kv),
+                (((1,), (1,)), ((), ())),
+                preferred_element_type=jnp.float32,
+            ).astype(out_ref.dtype)
+            for si in range(per_block):
+                at = si * shard + gi * half
+                out_ref[:, at:at + half] = part[:, si * half:(si + 1) * half]
 
     return pl.pallas_call(
         kernel,
         grid_spec=pltpu.PrefetchScalarGridSpec(
-            num_scalar_prefetch=2,
+            num_scalar_prefetch=3,
             grid=(d_model // block_rows,),
             in_specs=[
-                pl.BlockSpec((tokens, kv), lambda i, r, c: (0, 0)),
-                pl.BlockSpec((per_block, shard, kv), lambda i, r, c: (i, 0, 0)),
-                pl.BlockSpec((n, sub, kv), lambda i, r, c: (0, shard // sub, 0)),
+                pl.BlockSpec((tokens, kv), lambda i, r, c, g: (0, 0)),
+                pl.BlockSpec((halves, per_block, half, kv), lambda i, r, c, g: (0, i, 0, 0)),
+                pl.BlockSpec((1, n, sub, kv), lambda i, r, c, g: (g[0], 0, half // sub, 0)),
             ],
-            out_specs=pl.BlockSpec((tokens, block_rows), lambda i, r, c: (0, i)),
+            out_specs=pl.BlockSpec((tokens, block_rows), lambda i, r, c, g: (0, i)),
         ),
         out_shape=jax.ShapeDtypeStruct((tokens, d_model), jnp.bfloat16),
         interpret=interpret,
-    )(tile_rows, tile_cols, grad_values, gathered, gathered)
+    )(tile_rows, tile_cols, own_group, grad_values, gathered, gathered)
 
 
 def body(layer_input, grad_values, base_weight, tile_ids, tile_delta):
@@ -85,8 +91,13 @@
 
     sub = TILE * TILE // kv
     delta_rows = tile_delta.reshape(col_tiles, sub, TILE).transpose(1, 0, 2).reshape(sub, kv)
-    packed = jnp.concatenate([base_weight, delta_rows], axis=0)
-    gathered = lax.all_gather(packed, DP, axis=0, tiled=False)
+    groups = lax.axis_size("groups")
+    own_group = lax.axis_index("groups")
+    half = shard // groups
+    mine = lax.dynamic_slice_in_dim(base_weight, own_group * half, half, 0)
+    packed = jnp.concatenate([mine, delta_rows], axis=0)
+    gathered = lax.all_gather(packed, ("groups",) + DP, axis=0, tiled=False)
+    gathered = gathered.reshape(groups, n, half + sub, kv)
 
     all_ids = lax.all_to_all(jnp.broadcast_to(tile_ids, (n,)), DP, 0, 0, tiled=True)
     tile_rows = all_ids // col_tiles
@@ -107,7 +118,8 @@
     factor = 1.0 / math.sqrt(tokens_here * n)
     grad_tiles = jnp.sum(from_chips, axis=0, keepdims=True) * factor
 
-    grad_input = merged_matmul(tile_rows, tile_cols, grad_values, gathered, shard)
+    group_ids = jnp.reshape(own_group, (1,)).astype(jnp.int32)
+    grad_input = merged_matmul(tile_rows, tile_cols, group_ids, grad_values, gathered)
     return (grad_input, grad_tiles)
 
 

time: 138 us -> 167 us (1.21)
  waiting for transfers between devices: 45.1 us -> 64 us
  blocking collectives: 27.2 us -> 35.1 us
  local copies, waits for them, and re-layouts: 19.5 us -> 21.7 us
    all_gather x1, waiting for transfers between devices: 43.2 us -> 62.4 us  [body(): gathered = lax.all_gather(packed, ('groups',) + DP, axis=0, tiled=False)]
    all_to_all x1, blocking collectives: 27.2 us -> 35.1 us  [body(): from_chips = lax.all_to_all(chip_sum, 'chips', 0, 0, tiled=True)]
  transfers between devices with their start and end apart: 3 -> 3, of which waited for: 2 -> 2; matrix products, arithmetic and copies ran while one was open for 16% -> 15% of each run, Pallas kernels for 0% -> 0%
where the time goes in v4:
time: 167 us
  waiting for transfers between devices  64 us (38%)
  blocking collectives  35.1 us (21%)
  local copies, waits for them, and re-layouts  21.7 us (13%)
  Pallas kernels  17.4 us (10%)
  between operations  14.8 us (9%)
  starting transfers between devices  7.92 us (5%)
  other arithmetic  3.76 us (2%)
  matrix products  1.79 us (1%)
    all_gather x1, waiting for transfers between devices, body(): gathered = lax.all_gather(packed, ('groups',) + DP, axis=0, tiled=False)  62.4 us
    all_to_all x1, blocking collectives, body(): from_chips = lax.all_to_all(chip_sum, 'chips', 0, 0, tiled=True)  35.1 us
    pallas_call x1, Pallas kernels, merged_matmul(): pl.pallas_call(kernel, grid_spec=pltpu.PrefetchScalarGridSpec(num_scalar_...  17.4 us
    unnamed x6, local copies, waits for them, and re-layouts  8.96 us
    all_to_all x1, starting transfers between devices, body(): lax.all_to_all(jnp.broadcast_to(tile_ids, (n,)), DP, 0, 0, tiled=True)  7.41 us
    reshape x1, local copies, waits for them, and re-layouts, body(): input_panels = layer_input.reshape(tokens_here, row_tiles, TILE)  6.39 us
    gather x1, local copies, waits for them, and re-layouts, body(): rows_taken = jnp.take(input_panels, tile_rows, axis=1)  3.85 us
  transfers between devices with their start and end apart: 3, of which 2 were waited for; matrix products, arithmetic and copies ran while one was open for 15% of the time, Pallas kernels for 0%

profile of v4, /device:TPU:0, one launch (start us, length us, event | category | flops | bytes accessed | tf_op | source)
XLA Modules:
  0.0 166.5 jit_solution(18164498770037810786)
XLA Ops:
  7.2 0.0 all-gather.3.cloned.1.call-start
  7.2 0.8 copy.32
  8.1 0.3 copy-done
  8.4 0.9 pad_maximum_fusion
  9.3 0.0 all-gather.3.cloned.1.call-update
  10.0 0.6 broadcast_in_dim.27
  10.6 7.4 %all-to-all-start = ((s32[16,1,1]{2,1,0:T(1,128)}), s32[16,1,1]{2,1,0:T(1,128)S(1)}, u32[]{:S(2)}, u32[]{:S(2)}) async-start(s32[16,1,1]{2,1,0:T(1,128)} %broadcast_in_dim.27), calls=%async_computation | async-start | bytes 16384 | tf_op jit(solution)/shard_map/all_to_all | solution.py:102
  18.0 1.2 copy.26
  19.3 0.3 copy.27
  19.5 6.4 %copy.24 = bf16[256,8192]{0,1:T(8,128)(2,1)} copy(bf16[256,8192]{1,0:T(8,128)(2,1)} %param.5) | data formatting | bytes 8388608 | tf_op args[0]
  25.9 6.4 %copy.25 = bf16[256,64,128]{2,0,1:T(8,128)(2,1)} copy(bf16[256,64,128]{0,2,1:T(8,128)(2,1)} %bitcast.49) | data formatting | bytes 8388608 | tf_op jit(solution)/shard_map/reshape | solution.py:106
  32.3 0.4 reduce
  32.7 0.7 gather_fusion.1
  33.5 3.9 %gather_fusion = bf16[16,256,128]{2,1,0:T(8,128)(2,1)} fusion(bf16[256,64,128]{2,0,1:T(8,128)(2,1)} %copy.25, s32[1024]{0:T(1024)S(1)} %get-tuple-element.11), kind=kCustom, calls=%fused_computation | custom fusion | bytes 2097216 | tf_op jit(solution)/shard_map/jit(_take)/gather | solution.py:108
  37.4 0.6 compare_and_fusion
  37.9 1.8 %fusion = f32[16,128,128]{2,1,0:T(8,128)S(1)} fusion(bf16[16,256,128]{2,1,0:T(8,128)(2,1)S(1)} %gather_fusion.1, bf16[16,256,128]{2,1,0:T(8,128)(2,1)} %gather_fusion, pred[16]{0:T(512)(128)(4,1)S(1)} %get-tuple-element.4, pred[16]{0:T(512)(128)(4,1)S(1)} %get-tuple-element.8), kind=kOutput, calls=%fused_computation.2 | convolution fusion | flops 135266304 | bytes 3145760 | tf_op jit(solution)/shard_map/tja,tjb->jab/dot_general | solution.py:110
  39.8 1.0 copy-done.1
  40.8 0.5 collective-permute-start
  41.2 1.5 collective-permute-done
  42.8 1.3 bitcast_add_fusion
  44.0 35.1 %all_to_all.17 = f32[8,128,128]{2,1,0:T(8,128)S(1)} all-to-all(f32[8,128,128]{2,1,0:T(8,128)S(1)} %bitcast_add_fusion), channel_id=1, replica_groups=mesh['groups'=2,'chips'=8,'core'=2] {'chips'}, dimensions={0} | all-to-all | bytes 1048576 | tf_op jit(solution)/shard_map/all_to_all | solution.py:117
  79.2 0.6 multiply_bitcast_fusion
  79.8 62.4 %all-gather.3.cloned.1.call-done = bf16[8704,1024]{1,0:T(8,128)(2,1)} async-done(((bf16[272,1024]{1,0:T(8,128)(2,1)}), bf16[8704,1024]{1,0:T(8,128)(2,1)}) %all-gather.3.cloned.1.call-update) | async-done | bytes 17825808 | tf_op jit(solution)/shard_map/all_gather | solution.py:99
  142.2 17.4 %shard_map.68 = bf16[256,8192]{1,0:T(8,128)(2,1)} custom-call(s32[16]{0:T(128)} %get-tuple-element.9.rows_ref, s32[16]{0:T(128)} %get-tuple-element.5.cols_ref, s32[1]{0:T(128)} %bitcast.1.group_ref, bf16[256,1024]{1,0:T(8,128)(2,1)} %gv_ref.1, bf16[2,16,272,1024]{3,2,1,0:T(8,128)(2,1)} %bitcast.47, bf16[2,16,272,1024]{3,2,1,0:T(8,128)(2,1)} %bitcast.48), custom_call_target="tpu_custom_call" | custom-call | tf_op jit(solution)/shard_map/pallas_call | solution.py:65
  (8 shorter events, 0.1 us)
Async XLA Ops:
  7.2 1.2 copy-start
  7.2 135.1 %all-gather.3.cloned.1.call-start = ((), (), s32[]{:S(2)}) async-start(), calls=%async_computation.2 | async-start | bytes 18382848 | tf_op jit(solution)/shard_map/all_gather | solution.py:99
  10.6 21.7 %all-to-all-start = ((s32[16,1,1]{2,1,0:T(1,128)}), s32[16,1,1]{2,1,0:T(1,128)S(1)}, u32[]{:S(2)}, u32[]{:S(2)}) async-start(s32[16,1,1]{2,1,0:T(1,128)} %broadcast_in_dim.27), calls=%async_computation | async-start | bytes 16384 | tf_op jit(solution)/shard_map/all_to_all | solution.py:102
  39.7 1.0 copy-start.1
  40.8 2.0 %collective-permute-start = (f32[8,128,128]{2,1,0:T(8,128)S(1)}, f32[8,128,128]{2,1,0:T(8,128)S(1)}, u32[]{:S(2)}, u32[]{:S(2)}) collective-permute-start(f32[8,128,128]{2,1,0:T(8,128)S(1)} %dynamic-slice_bitcast_fusion), channel_id=1, source_target_pairs={{0,1},{1,0},{2,3},{3,2},{4,5},{5,4},{6,7},{7,6},{8,9},{9,8},{10,11... | collective-permute-start | bytes 1572872 | tf_op jit(solution)/shard_map/ppermute | solution.py:116
Sparse Core Ops, SparseCore 0:
  10.8 131.3 all-gather.2

commit v5 on v3

--- a/solution.py
+++ b/solution.py
@@ -32,16 +32,16 @@
             @pl.when((r >= 0) & (r < tiles_per_block))
             def _():
                 c = cols_ref[j]
-                for a in range(col_tiles):
-                    at = r * TILE + a * sub
-                    si = at // shard
-                    rs = pl.ds(pl.multiple_of(at % shard, sub), sub)
-                    add = delta_ref[j, :, a * TILE:(a + 1) * TILE].astype(jnp.float32)
-                    for cc in range(col_tiles):
+                for cc in range(col_tiles):
 
-                        @pl.when(c == cc)
-                        def _():
-                            cs = slice(cc * TILE, (cc + 1) * TILE)
+                    @pl.when(c == cc)
+                    def _():
+                        cs = slice(cc * TILE, (cc + 1) * TILE)
+                        for a in range(col_tiles):
+                            at = r * TILE + a * sub
+                            si = at // shard
+                            rs = pl.ds(pl.multiple_of(at % shard, sub), sub)
+                            add = delta_ref[j, :, a * TILE:(a + 1) * TILE].astype(jnp.float32)
                             cur = base_ref[si, rs, cs].astype(jnp.float32)
                             base_ref[si, rs, cs] = (cur + add).astype(jnp.bfloat16)
 

time: 138 us -> 135 us (0.978)
  Pallas kernels: 16 us -> 12.4 us
    pallas_call x1, Pallas kernels: 16 us -> 12.4 us  [merged_matmul(): pl.pallas_call(kernel, grid_spec=pltpu.PrefetchScalarGridSpec(num_scalar_...]
where the time goes in v5:
time: 135 us; the launch traced here: 133 us
  waiting for transfers between devices  45.1 us (33%)
  blocking collectives  27.2 us (20%)
  local copies, waits for them, and re-layouts  19.5 us (14%)
  between operations  14.8 us (11%)
  Pallas kernels  12.4 us (9%)
  starting transfers between devices  7.89 us (6%)
  other arithmetic  5.09 us (4%)
    all_gather x1, waiting for transfers between devices, body(): gathered = lax.all_gather(packed, DP, axis=0, tiled=False)  43.2 us
    all_to_all x1, blocking collectives, body(): from_chips = lax.all_to_all(chip_sum, 'chips', 0, 0, tiled=True)  27.2 us
    pallas_call x1, Pallas kernels, merged_matmul(): pl.pallas_call(kernel, grid_spec=pltpu.PrefetchScalarGridSpec(num_scalar_...  12.4 us
    unnamed x6, local copies, waits for them, and re-layouts  7.62 us
    all_to_all x1, starting transfers between devices, body(): lax.all_to_all(jnp.broadcast_to(tile_ids, (n,)), DP, 0, 0, tiled=True)  7.41 us
    reshape x1, local copies, waits for them, and re-layouts, body(): input_panels = layer_input.reshape(tokens_here, row_tiles, TILE)  6.39 us
    gather x1, local copies, waits for them, and re-layouts, body(): rows_taken = jnp.take(input_panels, tile_rows, axis=1)  3.07 us
  transfers between devices with their start and end apart: 3, of which 2 were waited for; matrix products, arithmetic and copies ran while one was open for 16% of the time, Pallas kernels for 0%

profile of v5, /device:TPU:0, one launch (start us, length us, event | category | flops | bytes accessed | tf_op | source)
XLA Modules:
  0.0 132.6 jit_solution(5421559422076957928)
XLA Ops:
  7.2 0.0 copy-start
  7.2 0.0 all-gather.3.cloned.1.call-start
  7.2 0.8 copy.32
  8.0 2.3 %pad_maximum_fusion = bf16[528,1024]{1,0:T(8,128)(2,1)} fusion(bf16[16,1024]{1,0:T(8,128)(2,1)S(1)} %bitcast.52, bf16[512,1024]{1,0:T(8,128)(2,1)} %param.7), kind=kLoop, calls=%fused_computation.2 | loop fusion | flops 2162688 | bytes 2162688 | tf_op jit(solution)/shard_map/concatenate | solution.py:88
  10.4 0.0 all-gather.3.cloned.1.call-update
  11.0 0.6 broadcast_in_dim.27
  11.6 7.4 %all-to-all-start = ((s32[16,1,1]{2,1,0:T(1,128)}), s32[16,1,1]{2,1,0:T(1,128)S(1)}, u32[]{:S(2)}, u32[]{:S(2)}) async-start(s32[16,1,1]{2,1,0:T(1,128)} %broadcast_in_dim.27), calls=%async_computation | async-start | bytes 16384 | tf_op jit(solution)/shard_map/all_to_all | solution.py:91
  19.1 0.2 copy.26
  19.3 0.3 copy.27
  19.6 6.4 %copy.24 = bf16[256,8192]{0,1:T(8,128)(2,1)} copy(bf16[256,8192]{1,0:T(8,128)(2,1)} %param.5) | data formatting | bytes 8388608 | tf_op args[0]
  26.0 6.4 %copy.25 = bf16[256,64,128]{2,0,1:T(8,128)(2,1)} copy(bf16[256,64,128]{0,2,1:T(8,128)(2,1)} %bitcast.48) | data formatting | bytes 8388608 | tf_op jit(solution)/shard_map/reshape | solution.py:95
  32.4 0.4 reduce
  32.8 0.7 gather_fusion.1
  33.6 3.1 %gather_fusion = bf16[16,256,128]{2,1,0:T(8,128)(2,1)S(1)} fusion(bf16[256,64,128]{2,0,1:T(8,128)(2,1)} %copy.25, s32[1024]{0:T(1024)S(1)} %get-tuple-element.11), kind=kCustom, calls=%fused_computation | custom fusion | bytes 2097216 | tf_op jit(solution)/shard_map/jit(_take)/gather | solution.py:97
  36.6 0.6 compare_and_fusion
  37.2 0.6 fusion
  37.8 1.0 copy-done.1
  38.8 0.4 collective-permute-start
  39.3 1.9 %collective-permute-done = f32[8,128,128]{2,1,0:T(8,128)S(1)} collective-permute-done((f32[8,128,128]{2,1,0:T(8,128)S(1)}, f32[8,128,128]{2,1,0:T(8,128)S(1)}, u32[]{:S(2)}, u32[]{:S(2)}) %collective-permute-start) | collective-permute-done | bytes 524320 | tf_op jit(solution)/shard_map/ppermute | solution.py:105
  41.2 1.1 bitcast_add_fusion
  42.3 27.2 %all_to_all.17 = f32[8,128,128]{2,1,0:T(8,128)S(1)} all-to-all(f32[8,128,128]{2,1,0:T(8,128)S(1)} %bitcast_add_fusion), channel_id=1, replica_groups=mesh['groups'=2,'chips'=8,'core'=2] {'chips'}, dimensions={0} | all-to-all | bytes 1048576 | tf_op jit(solution)/shard_map/all_to_all | solution.py:106
  69.5 0.6 multiply_bitcast_fusion
  70.1 43.2 %all-gather.3.cloned.1.call-done = bf16[8448,1024]{1,0:T(8,128)(2,1)} async-done(((bf16[528,1024]{1,0:T(8,128)(2,1)}), bf16[8448,1024]{1,0:T(8,128)(2,1)}) %all-gather.3.cloned.1.call-update) | async-done | bytes 17301520 | tf_op jit(solution)/shard_map/all_gather | solution.py:89
  113.3 12.4 %shard_map.68 = bf16[256,8192]{1,0:T(8,128)(2,1)} custom-call(s32[16]{0:T(128)} %get-tuple-element.9.rows_ref, s32[16]{0:T(128)} %get-tuple-element.5.cols_ref, bf16[256,1024]{1,0:T(8,128)(2,1)} %gv_ref.1, bf16[16,528,1024]{2,1,0:T(8,128)(2,1)} %bitcast.46, bf16[16,528,1024]{2,1,0:T(8,128)(2,1)} %bitcast.47), custom_call_target="tpu_custom_call" | custom-call | tf_op jit(solution)/shard_map/pallas_call | solution.py:59
  (7 shorter events, 0.1 us)
Async XLA Ops:
  7.2 11.9 %copy-start = (bf16[256,1024]{1,0:T(8,128)(2,1)S(1)}, bf16[256,1024]{1,0:T(8,128)(2,1)}, u32[]{:S(2)}) copy-start(bf16[256,1024]{1,0:T(8,128)(2,1)} %gv_ref.1) | copy-start | bytes 1572868
  7.2 106.1 %all-gather.3.cloned.1.call-start = ((), (), s32[]{:S(2)}) async-start(), calls=%async_computation.2 | async-start | bytes 18382848 | tf_op jit(solution)/shard_map/all_gather | solution.py:89
  11.6 20.8 %all-to-all-start = ((s32[16,1,1]{2,1,0:T(1,128)}), s32[16,1,1]{2,1,0:T(1,128)S(1)}, u32[]{:S(2)}, u32[]{:S(2)}) async-start(s32[16,1,1]{2,1,0:T(1,128)} %broadcast_in_dim.27), calls=%async_computation | async-start | bytes 16384 | tf_op jit(solution)/shard_map/all_to_all | solution.py:91
  37.8 1.0 copy-start.1
  38.8 2.3 %collective-permute-start = (f32[8,128,128]{2,1,0:T(8,128)S(1)}, f32[8,128,128]{2,1,0:T(8,128)S(1)}, u32[]{:S(2)}, u32[]{:S(2)}) collective-permute-start(f32[8,128,128]{2,1,0:T(8,128)S(1)} %dynamic-slice_bitcast_fusion), channel_id=1, source_target_pairs={{0,1},{1,0},{2,3},{3,2},{4,5},{5,4},{6,7},{7,6},{8,9},{9,8},{10,11... | collective-permute-start | bytes 1572872 | tf_op jit(solution)/shard_map/ppermute | solution.py:105
Sparse Core Ops, SparseCore 0:
  10.5 102.7 all-gather.2

commit v6 on v5

--- a/solution.py
+++ b/solution.py
@@ -13,14 +13,12 @@
 DP = ("chips", "core")
 
 
-def merged_matmul(tile_rows, tile_cols, grad_values, gathered, shard, interpret=False):
+def merged_matmul(tile_rows, tile_cols, grad_values, full_base, all_delta_rows, interpret=False):
     tokens, kv = grad_values.shape
-    n, packed_rows, _ = gathered.shape
-    sub = packed_rows - shard
-    d_model = n * shard
+    d_model = full_base.shape[0]
+    n, sub, _ = all_delta_rows.shape
     col_tiles = kv // TILE
-    block_rows = max(min(BLOCK_ROWS, d_model), shard)
-    per_block = block_rows // shard
+    block_rows = min(BLOCK_ROWS, d_model)
     tiles_per_block = block_rows // TILE
 
     def kernel(rows_ref, cols_ref, gv_ref, base_ref, delta_ref, out_ref):
@@ -38,20 +36,17 @@
                     def _():
                         cs = slice(cc * TILE, (cc + 1) * TILE)
                         for a in range(col_tiles):
-                            at = r * TILE + a * sub
-                            si = at // shard
-                            rs = pl.ds(pl.multiple_of(at % shard, sub), sub)
+                            rs = pl.ds(pl.multiple_of(r * TILE + a * sub, sub), sub)
                             add = delta_ref[j, :, a * TILE:(a + 1) * TILE].astype(jnp.float32)
-                            cur = base_ref[si, rs, cs].astype(jnp.float32)
-                            base_ref[si, rs, cs] = (cur + add).astype(jnp.bfloat16)
+                            cur = base_ref[rs, cs].astype(jnp.float32)
+                            base_ref[rs, cs] = (cur + add).astype(jnp.bfloat16)
 
             return carry
 
         lax.fori_loop(0, n, patch, 0)
-        merged = base_ref[...].reshape(block_rows, kv)
         out_ref[...] = lax.dot_general(
             gv_ref[...],
-            merged,
+            base_ref[...],
             (((1,), (1,)), ((), ())),
             preferred_element_type=jnp.float32,
         ).astype(out_ref.dtype)
@@ -63,14 +58,14 @@
             grid=(d_model // block_rows,),
             in_specs=[
                 pl.BlockSpec((tokens, kv), lambda i, r, c: (0, 0)),
-                pl.BlockSpec((per_block, shard, kv), lambda i, r, c: (i, 0, 0)),
-                pl.BlockSpec((n, sub, kv), lambda i, r, c: (0, shard // sub, 0)),
+                pl.BlockSpec((block_rows, kv), lambda i, r, c: (i, 0)),
+                pl.BlockSpec((n, sub, kv), lambda i, r, c: (0, 0, 0)),
             ],
             out_specs=pl.BlockSpec((tokens, block_rows), lambda i, r, c: (0, i)),
         ),
         out_shape=jax.ShapeDtypeStruct((tokens, d_model), jnp.bfloat16),
         interpret=interpret,
-    )(tile_rows, tile_cols, grad_values, gathered, gathered)
+    )(tile_rows, tile_cols, grad_values, full_base, all_delta_rows)
 
 
 def body(layer_input, grad_values, base_weight, tile_ids, tile_delta):
@@ -85,8 +80,8 @@
 
     sub = TILE * TILE // kv
     delta_rows = tile_delta.reshape(col_tiles, sub, TILE).transpose(1, 0, 2).reshape(sub, kv)
-    packed = jnp.concatenate([base_weight, delta_rows], axis=0)
-    gathered = lax.all_gather(packed, DP, axis=0, tiled=False)
+    full_base = lax.all_gather(base_weight, DP, axis=0, tiled=True)
+    all_delta_rows = lax.all_gather(delta_rows, DP, axis=0, tiled=False)
 
     all_ids = lax.all_to_all(jnp.broadcast_to(tile_ids, (n,)), DP, 0, 0, tiled=True)
     tile_rows = all_ids // col_tiles
@@ -107,7 +102,7 @@
     factor = 1.0 / math.sqrt(tokens_here * n)
     grad_tiles = jnp.sum(from_chips, axis=0, keepdims=True) * factor
 
-    grad_input = merged_matmul(tile_rows, tile_cols, grad_values, gathered, shard)
+    grad_input = merged_matmul(tile_rows, tile_cols, grad_values, full_base, all_delta_rows)
     return (grad_input, grad_tiles)
 
 

time: 135 us -> 170 us (1.26); the launches traced: 133 us -> 170 us
  waiting for transfers between devices: 45.1 us -> 67.6 us
  blocking collectives: 27.2 us -> 37.7 us
  starting transfers between devices: 7.89 us -> 13.8 us
    all_gather x0 -> x1, blocking collectives: none -> 37.7 us  [body(): all_delta_rows = lax.all_gather(delta_rows, DP, axis=0, tiled=False)]
    all_to_all x1 -> x0, blocking collectives: 27.2 us -> none  [body(): from_chips = lax.all_to_all(chip_sum, 'chips', 0, 0, tiled=True)]
    all_gather x1, waiting for transfers between devices: 43.2 us -> 65.4 us  [body(): full_base = lax.all_gather(base_weight, DP, axis=0, tiled=True)]
    all_to_all x0 -> x1, starting transfers between devices: none -> 5.9 us  [body(): from_chips = lax.all_to_all(chip_sum, 'chips', 0, 0, tiled=True)]
    concatenate x1 -> x0, other arithmetic: 2.32 us -> none  [body(): packed = jnp.concatenate([base_weight, delta_rows], axis=0)]
  transfers between devices with their start and end apart: 3 -> 4, of which waited for: 2 -> 2; matrix products, arithmetic and copies ran while one was open for 16% -> 13% of each run, Pallas kernels for 0% -> 0%
where the time goes in v6:
time: 170 us
  waiting for transfers between devices  67.6 us (40%)
  blocking collectives  37.7 us (22%)
  local copies, waits for them, and re-layouts  19.8 us (12%)
  between operations  14.8 us (9%)
  starting transfers between devices  13.8 us (8%)
  Pallas kernels  12 us (7%)
  other arithmetic  3.52 us (2%)
    all_gather x1, waiting for transfers between devices, body(): full_base = lax.all_gather(base_weight, DP, axis=0, tiled=True)  65.4 us
    all_gather x1, blocking collectives, body(): all_delta_rows = lax.all_gather(delta_rows, DP, axis=0, tiled=False)  37.7 us
    pallas_call x1, Pallas kernels, merged_matmul(): pl.pallas_call(kernel, grid_spec=pltpu.PrefetchScalarGridSpec(num_scalar_...  12 us
    unnamed x6, local copies, waits for them, and re-layouts  8.77 us
    all_to_all x1, starting transfers between devices, body(): lax.all_to_all(jnp.broadcast_to(tile_ids, (n,)), DP, 0, 0, tiled=True)  7.41 us
    reshape x1, local copies, waits for them, and re-layouts, body(): input_panels = layer_input.reshape(tokens_here, row_tiles, TILE)  6.35 us
    all_to_all x1, starting transfers between devices, body(): from_chips = lax.all_to_all(chip_sum, 'chips', 0, 0, tiled=True)  5.9 us
  transfers between devices with their start and end apart: 4, of which 2 were waited for; matrix products, arithmetic and copies ran while one was open for 13% of the time, Pallas kernels for 0%

profile of v6, /device:TPU:0, one launch (start us, length us, event | category | flops | bytes accessed | tf_op | source)
XLA Modules:
  0.0 169.8 jit_solution(5586676924486331422)
XLA Ops:
  7.2 0.0 all-gather.2.cloned.1.call-start
  7.2 0.7 all-gather.2.cloned.1.call-update
  8.5 0.6 broadcast_in_dim.27
  9.1 7.4 %all-to-all-start = ((s32[16,1,1]{2,1,0:T(1,128)}), s32[16,1,1]{2,1,0:T(1,128)S(1)}, u32[]{:S(2)}, u32[]{:S(2)}) async-start(s32[16,1,1]{2,1,0:T(1,128)} %broadcast_in_dim.27), calls=%async_computation | async-start | bytes 16384 | tf_op jit(solution)/shard_map/all_to_all | solution.py:86
  16.6 1.2 copy.26
  17.8 0.3 copy.27
  18.1 6.5 %copy.24 = bf16[256,8192]{0,1:T(8,128)(2,1)} copy(bf16[256,8192]{1,0:T(8,128)(2,1)} %param.5) | data formatting | bytes 8388608 | tf_op args[0]
  24.6 6.4 %copy.25 = bf16[256,64,128]{2,0,1:T(8,128)(2,1)} copy(bf16[256,64,128]{0,2,1:T(8,128)(2,1)} %bitcast.42) | data formatting | bytes 8388608 | tf_op jit(solution)/shard_map/reshape | solution.py:90
  31.0 0.4 reduce
  31.4 0.7 gather_fusion.1
  32.2 3.0 %gather_fusion = bf16[16,256,128]{2,1,0:T(8,128)(2,1)S(1)} fusion(bf16[256,64,128]{2,0,1:T(8,128)(2,1)} %copy.25, s32[1024]{0:T(1024)S(1)} %get-tuple-element.11), kind=kCustom, calls=%fused_computation | custom fusion | bytes 2097216 | tf_op jit(solution)/shard_map/jit(_take)/gather | solution.py:92
  35.2 0.0 copy-start.1
  35.2 0.6 compare_and_fusion
  35.7 0.6 fusion
  36.3 0.0 copy-start
  36.3 1.0 copy-done
  37.3 0.5 collective-permute-start
  37.8 1.5 collective-permute-done
  39.3 1.9 %bitcast_add_fusion = f32[8,128,128]{2,1,0:T(8,128)} fusion(f32[8,128,128]{2,1,0:T(8,128)S(1)} %collective-permute-done, f32[8,2,128,128]{3,2,1,0:T(8,128)} %bitcast.45, s32[]{:T(128)S(6)} %select_n.71), kind=kLoop, calls=%fused_computation.9 | loop fusion | flops 131072 | bytes 1572868 | tf_op jit(solution)/shard_map/add | solution.py:100
  41.2 5.9 %all-to-all-start.1 = ((f32[8,128,128]{2,1,0:T(8,128)}), f32[8,128,128]{2,1,0:T(8,128)S(1)}, u32[]{:S(2)}, u32[]{:S(2)}) async-start(f32[8,128,128]{2,1,0:T(8,128)} %bitcast_add_fusion), calls=%async_computation.1 | async-start | bytes 1048576 | tf_op jit(solution)/shard_map/all_to_all | solution.py:101
  47.2 37.7 %all_gather.7.delta_ref = bf16[16,16,1024]{2,1,0:T(8,128)(2,1)} all-gather(bf16[1,16,1024]{2,1,0:T(8,128)(2,1)S(1)} %all_gather_reshape.3), channel_id=1, replica_groups=mesh['groups'=2,'chips'=8,'core'=2] {'chips','core'}, dimensions={0}, use_global_device_ids=true | all-gather | bytes 557056 | tf_op jit(solution)/shard_map/all_gather | solution.py:84
  84.9 0.6 multiply_bitcast_fusion
  85.5 65.4 %all-gather.2.cloned.1.call-done.base_ref = bf16[8192,1024]{1,0:T(8,128)(2,1)} async-done(((bf16[512,1024]{1,0:T(8,128)(2,1)}), bf16[8192,1024]{1,0:T(8,128)(2,1)}) %all-gather.2.cloned.1.call-update) | async-done | bytes 16777232 | tf_op jit(solution)/shard_map/all_gather | solution.py:83
  150.9 12.0 %shard_map.68 = bf16[256,8192]{1,0:T(8,128)(2,1)} custom-call(s32[16]{0:T(128)} %get-tuple-element.9.rows_ref, s32[16]{0:T(128)} %get-tuple-element.5.cols_ref, bf16[256,1024]{1,0:T(8,128)(2,1)} %gv_ref.1, bf16[8192,1024]{1,0:T(8,128)(2,1)} %all-gather.2.cloned.1.call-done.base_ref, bf16[16,16,1024]{2,1,0:T(8,128)(2,1)} %all_gather.7.delta_ref), custom_call_target="tpu_custom_call" | custom-call | tf_op jit(solution)/shard_map/pallas_call | solution.py:54
  (9 shorter events, 0.1 us)
Async XLA Ops:
  7.2 143.8 %all-gather.2.cloned.1.call-start = ((), (), s32[]{:S(2)}) async-start(), calls=%async_computation.2 | async-start | bytes 17825792 | tf_op jit(solution)/shard_map/all_gather | solution.py:83
  9.1 21.9 %all-to-all-start = ((s32[16,1,1]{2,1,0:T(1,128)}), s32[16,1,1]{2,1,0:T(1,128)S(1)}, u32[]{:S(2)}, u32[]{:S(2)}) async-start(s32[16,1,1]{2,1,0:T(1,128)} %broadcast_in_dim.27), calls=%async_computation | async-start | bytes 16384 | tf_op jit(solution)/shard_map/all_to_all | solution.py:86
  35.2 12.0 %copy-start.1 = (bf16[1,128,128]{2,1,0:T(8,128)(2,1)S(1)}, bf16[1,128,128]{2,1,0:T(8,128)(2,1)}, u32[]{:S(2)}) copy-start(bf16[1,128,128]{2,1,0:T(8,128)(2,1)} %param.9) | copy-start | bytes 98308
  36.3 1.0 copy-start
  37.3 2.0 %collective-permute-start = (f32[8,128,128]{2,1,0:T(8,128)S(1)}, f32[8,128,128]{2,1,0:T(8,128)S(1)}, u32[]{:S(2)}, u32[]{:S(2)}) collective-permute-start(f32[8,128,128]{2,1,0:T(8,128)S(1)} %dynamic-slice_bitcast_fusion), channel_id=1, source_target_pairs={{0,1},{1,0},{2,3},{3,2},{4,5},{5,4},{6,7},{7,6},{8,9},{9,8},{10,11... | collective-permute-start | bytes 1572872 | tf_op jit(solution)/shard_map/ppermute | solution.py:100
  41.2 43.6 %all-to-all-start.1 = ((f32[8,128,128]{2,1,0:T(8,128)}), f32[8,128,128]{2,1,0:T(8,128)S(1)}, u32[]{:S(2)}, u32[]{:S(2)}) async-start(f32[8,128,128]{2,1,0:T(8,128)} %bitcast_add_fusion), calls=%async_computation.1 | async-start | bytes 1048576 | tf_op jit(solution)/shard_map/all_to_all | solution.py:101
Sparse Core Ops, SparseCore 0:
  10.1 140.7 all-gather.1

commit v7 on v5

--- a/solution.py
+++ b/solution.py
@@ -73,6 +73,30 @@
     )(tile_rows, tile_cols, grad_values, gathered, gathered)
 
 
+def tile_partials(tile_rows, tile_cols, layer_input, grad_values):
+    tokens = layer_input.shape[0]
+    listed = tile_rows.shape[0]
+
+    def kernel(rows_ref, cols_ref, x_ref, g_ref, o_ref):
+        o_ref[0] = jnp.dot(
+            x_ref[...].T, g_ref[...], preferred_element_type=jnp.float32
+        )
+
+    return pl.pallas_call(
+        kernel,
+        grid_spec=pltpu.PrefetchScalarGridSpec(
+            num_scalar_prefetch=2,
+            grid=(listed,),
+            in_specs=[
+                pl.BlockSpec((tokens, TILE), lambda j, r, c: (0, r[j])),
+                pl.BlockSpec((tokens, TILE), lambda j, r, c: (0, c[j])),
+            ],
+            out_specs=pl.BlockSpec((1, TILE, TILE), lambda j, r, c: (j, 0, 0)),
+        ),
+        out_shape=jax.ShapeDtypeStruct((listed, TILE, TILE), jnp.float32),
+    )(tile_rows, tile_cols, layer_input, grad_values)
+
+
 def body(layer_input, grad_values, base_weight, tile_ids, tile_delta):
     chips = lax.axis_size("chips")
     n = 2 * chips
@@ -92,17 +116,13 @@
     tile_rows = all_ids // col_tiles
     tile_cols = all_ids % col_tiles
 
-    input_panels = layer_input.reshape(tokens_here, row_tiles, TILE)
-    grad_panels = grad_values.reshape(tokens_here, col_tiles, TILE)
-    rows_taken = jnp.take(input_panels, tile_rows, axis=1)
-    cols_taken = jnp.take(grad_panels, tile_cols, axis=1)
-    partial = jnp.einsum(
-        "tja,tjb->jab", rows_taken, cols_taken, preferred_element_type=jnp.float32
-    ).reshape(chips, 2, TILE, TILE)
+    partial = tile_partials(tile_rows, tile_cols, layer_input, grad_values)
+    partial = partial.reshape(chips, 2, TILE, TILE)
     core = lax.axis_index("core")
     mine = lax.dynamic_index_in_dim(partial, core, axis=1, keepdims=False)
     other = lax.dynamic_index_in_dim(partial, 1 - core, axis=1, keepdims=False)
     chip_sum = mine + lax.ppermute(other, "core", [(0, 1), (1, 0)])
+    gathered, chip_sum = lax.optimization_barrier((gathered, chip_sum))
     from_chips = lax.all_to_all(chip_sum, "chips", 0, 0, tiled=True)
     factor = 1.0 / math.sqrt(tokens_here * n)
     grad_tiles = jnp.sum(from_chips, axis=0, keepdims=True) * factor

time: 135 us -> 133 us (0.985)
  waiting for transfers between devices: 45.1 us -> 73.4 us
  blocking collectives: 27.2 us -> 0 us
  local copies, waits for them, and re-layouts: 19.5 us -> 2.51 us
  Pallas kernels: 12.4 us -> 23.3 us
  starting transfers between devices: 7.89 us -> 12.1 us
    all_to_all x1 -> x0, blocking collectives: 27.2 us -> none  [body(): from_chips = lax.all_to_all(chip_sum, 'chips', 0, 0, tiled=True)]
    all_gather x1, waiting for transfers between devices: 43.2 us -> 62.3 us  [body(): gathered = lax.all_gather(packed, DP, axis=0, tiled=False)]
    pallas_call x0 -> x1, Pallas kernels: none -> 10.9 us  [tile_partials(): pl.pallas_call(kernel, grid_spec=pltpu.PrefetchScalarGridSpec(num_scalar_...]
    unnamed x6 -> x0, local copies, waits for them, and re-layouts: 7.62 us -> none
    reshape x2 -> x0, local copies, waits for them, and re-layouts: 6.66 us -> none  [the longest x1 6.39 us: body(): input_panels = layer_input.reshape(tokens_here, row_tiles, TILE)]
    all_to_all x1, waiting for transfers between devices: 0.01 us -> 6.36 us  [body(): lax.all_to_all(jnp.broadcast_to(tile_ids, (n,)), DP, 0, 0, tiled=True)]
    all_to_all x0 -> x1, starting transfers between devices: none -> 4.57 us  [body(): from_chips = lax.all_to_all(chip_sum, 'chips', 0, 0, tiled=True)]
    gather x2 -> x0, local copies, waits for them, and re-layouts: 3.82 us -> none  [the longest x1 3.07 us: body(): rows_taken = jnp.take(input_panels, tile_rows, axis=1)]
  transfers between devices with their start and end apart: 3 -> 4, of which waited for: 2 -> 4; matrix products, arithmetic and copies ran while one was open for 16% -> 3% of each run, Pallas kernels for 0% -> 18%
where the time goes in v7:
time: 133 us; the launch traced here: 132 us
  waiting for transfers between devices  73.4 us (55%)
  Pallas kernels  23.3 us (18%)
  between operations  14.7 us (11%)
  starting transfers between devices  12.1 us (9%)
  other arithmetic  5.76 us (4%)
  local copies, waits for them, and re-layouts  2.51 us (2%)
    all_gather x1, waiting for transfers between devices, body(): gathered = lax.all_gather(packed, DP, axis=0, tiled=False)  62.3 us
    pallas_call x1, Pallas kernels, merged_matmul(): pl.pallas_call(kernel, grid_spec=pltpu.PrefetchScalarGridSpec(num_scalar_...  12.4 us
    pallas_call x1, Pallas kernels, tile_partials(): pl.pallas_call(kernel, grid_spec=pltpu.PrefetchScalarGridSpec(num_scalar_...  10.9 us
    all_to_all x1, starting transfers between devices, body(): lax.all_to_all(jnp.broadcast_to(tile_ids, (n,)), DP, 0, 0, tiled=True)  7.41 us
    all_to_all x1, waiting for transfers between devices, body(): lax.all_to_all(jnp.broadcast_to(tile_ids, (n,)), DP, 0, 0, tiled=True)  6.36 us
    all_to_all x1, starting transfers between devices, body(): from_chips = lax.all_to_all(chip_sum, 'chips', 0, 0, tiled=True)  4.57 us
  transfers between devices with their start and end apart: 4, of which 4 were waited for; matrix products, arithmetic and copies ran while one was open for 3% of the time, Pallas kernels for 18%

profile of v7, /device:TPU:0, one launch (start us, length us, event | category | flops | bytes accessed | tf_op | source)
XLA Modules:
  0.0 131.8 jit_solution(3218506009815775890)
XLA Ops:
  7.2 0.0 all-gather.3.cloned.1.call-start
  7.2 0.8 copy.12
  8.0 2.3 %pad_maximum_fusion = bf16[528,1024]{1,0:T(8,128)(2,1)} fusion(bf16[16,1024]{1,0:T(8,128)(2,1)S(1)} %bitcast.21, bf16[512,1024]{1,0:T(8,128)(2,1)} %param.7), kind=kLoop, calls=%fused_computation | loop fusion | flops 2162688 | bytes 2162688 | tf_op jit(solution)/shard_map/concatenate | solution.py:112
  10.2 0.0 all-gather.3.cloned.1.call-update
  10.9 0.6 broadcast_in_dim.9
  11.5 7.4 %all-to-all-start = ((s32[16,1,1]{2,1,0:T(1,128)}), s32[16,1,1]{2,1,0:T(1,128)S(1)}, u32[]{:S(2)}, u32[]{:S(2)}) async-start(s32[16,1,1]{2,1,0:T(1,128)} %broadcast_in_dim.9), calls=%async_computation | async-start | bytes 16384 | tf_op jit(solution)/shard_map/all_to_all | solution.py:115
  19.0 6.4 %all-to-all-done = s32[16,1,1]{2,1,0:T(1,128)S(1)} async-done(((s32[16,1,1]{2,1,0:T(1,128)}), s32[16,1,1]{2,1,0:T(1,128)S(1)}, u32[]{:S(2)}, u32[]{:S(2)}) %all-to-all-start) | async-done | bytes 96 | tf_op jit(solution)/shard_map/all_to_all | solution.py:115
  25.3 0.4 reduce
  25.7 0.5 and_select_fusion
  26.2 10.9 %shard_map.68 = f32[16,128,128]{2,1,0:T(8,128)} custom-call(s32[16]{0:T(128)} %get-tuple-element.7.rows_ref, s32[16]{0:T(128)} %get-tuple-element.6.cols_ref, bf16[256,8192]{1,0:T(8,128)(2,1)} %x_ref.1, bf16[256,1024]{1,0:T(8,128)(2,1)} %gv_ref.1), custom_call_target="tpu_custom_call" | custom-call | tf_op jit(solution)/shard_map/pallas_call | solution.py:85
  37.1 1.1 dynamic-slice_bitcast_fusion
  38.3 0.1 collective-permute-start
  38.3 2.2 %collective-permute-done = f32[8,128,128]{2,1,0:T(8,128)S(1)} collective-permute-done((f32[8,128,128]{2,1,0:T(8,128)S(1)}, f32[8,128,128]{2,1,0:T(8,128)S(1)}, u32[]{:S(2)}, u32[]{:S(2)}) %collective-permute-start) | collective-permute-done | bytes 524320 | tf_op jit(solution)/shard_map/ppermute | solution.py:124
  40.5 1.9 %bitcast_add_fusion = f32[8,128,128]{2,1,0:T(8,128)} fusion(f32[8,128,128]{2,1,0:T(8,128)S(1)} %collective-permute-done, f32[8,2,128,128]{3,2,1,0:T(8,128)} %bitcast.20, s32[]{:T(128)S(6)} %select_n.21), kind=kLoop, calls=%fused_computation.1 | loop fusion | flops 131072 | bytes 1572868 | tf_op jit(solution)/shard_map/add | solution.py:124
  42.4 62.3 %all-gather.3.cloned.1.call-done = bf16[8448,1024]{1,0:T(8,128)(2,1)} async-done(((bf16[528,1024]{1,0:T(8,128)(2,1)}), bf16[8448,1024]{1,0:T(8,128)(2,1)}) %all-gather.3.cloned.1.call-update) | async-done | bytes 17301520 | tf_op jit(solution)/shard_map/all_gather | solution.py:113
  104.8 4.6 %all-to-all-start.1 = ((f32[8,128,128]{2,1,0:T(8,128)}), f32[8,128,128]{2,1,0:T(8,128)S(1)}, u32[]{:S(2)}, u32[]{:S(2)}) async-start(f32[8,128,128]{2,1,0:T(8,128)} %bitcast_add_fusion), calls=%async_computation.1 | async-start | bytes 1048576 | tf_op jit(solution)/shard_map/all_to_all | solution.py:126
  109.3 12.4 %shard_map.69 = bf16[256,8192]{1,0:T(8,128)(2,1)} custom-call(s32[16]{0:T(128)} %get-tuple-element.7.rows_ref, s32[16]{0:T(128)} %get-tuple-element.6.cols_ref, bf16[256,1024]{1,0:T(8,128)(2,1)} %gv_ref.1, bf16[16,528,1024]{2,1,0:T(8,128)(2,1)} %bitcast.17, bf16[16,528,1024]{2,1,0:T(8,128)(2,1)} %bitcast.18), custom_call_target="tpu_custom_call" | custom-call | tf_op jit(solution)/shard_map/pallas_call | solution.py:59
  121.8 2.5 %all-to-all-done.1 = f32[8,128,128]{2,1,0:T(8,128)S(1)} async-done(((f32[8,128,128]{2,1,0:T(8,128)}), f32[8,128,128]{2,1,0:T(8,128)S(1)}, u32[]{:S(2)}, u32[]{:S(2)}) %all-to-all-start.1) | async-done | bytes 524320 | tf_op jit(solution)/shard_map/all_to_all | solution.py:126
  124.3 0.6 multiply_bitcast_fusion
  (1 shorter events, 0.0 us)
Async XLA Ops:
  7.2 97.6 %all-gather.3.cloned.1.call-start = ((), (), s32[]{:S(2)}) async-start(), calls=%async_computation.2 | async-start | bytes 18382848 | tf_op jit(solution)/shard_map/all_gather | solution.py:113
  11.5 13.8 %all-to-all-start = ((s32[16,1,1]{2,1,0:T(1,128)}), s32[16,1,1]{2,1,0:T(1,128)S(1)}, u32[]{:S(2)}, u32[]{:S(2)}) async-start(s32[16,1,1]{2,1,0:T(1,128)} %broadcast_in_dim.9), calls=%async_computation | async-start | bytes 16384 | tf_op jit(solution)/shard_map/all_to_all | solution.py:115
  38.3 2.3 %collective-permute-start = (f32[8,128,128]{2,1,0:T(8,128)S(1)}, f32[8,128,128]{2,1,0:T(8,128)S(1)}, u32[]{:S(2)}, u32[]{:S(2)}) collective-permute-start(f32[8,128,128]{2,1,0:T(8,128)S(1)} %dynamic-slice_bitcast_fusion), channel_id=1, source_target_pairs={{0,1},{1,0},{2,3},{3,2},{4,5},{5,4},{6,7},{7,6},{8,9},{9,8},{10,11... | collective-permute-start | bytes 1572872 | tf_op jit(solution)/shard_map/ppermute | solution.py:124
  104.8 19.5 %all-to-all-start.1 = ((f32[8,128,128]{2,1,0:T(8,128)}), f32[8,128,128]{2,1,0:T(8,128)S(1)}, u32[]{:S(2)}, u32[]{:S(2)}) async-start(f32[8,128,128]{2,1,0:T(8,128)} %bitcast_add_fusion), calls=%async_computation.1 | async-start | bytes 1048576 | tf_op jit(solution)/shard_map/all_to_all | solution.py:126
Sparse Core Ops, SparseCore 0:
  10.4 94.3 all-gather.2

commit v8 on v7

--- a/solution.py
+++ b/solution.py
@@ -73,6 +73,27 @@
     )(tile_rows, tile_cols, grad_values, gathered, gathered)
 
 
+def packed_shard(base_weight, delta_rows):
+    rows, kv = base_weight.shape
+    sub = delta_rows.shape[0]
+
+    def kernel(b_ref, d_ref, o_ref, sem):
+        first = pltpu.make_async_copy(b_ref, o_ref.at[pl.ds(0, rows)], sem.at[0])
+        second = pltpu.make_async_copy(d_ref, o_ref.at[pl.ds(rows, sub)], sem.at[1])
+        first.start()
+        second.start()
+        first.wait()
+        second.wait()
+
+    return pl.pallas_call(
+        kernel,
+        in_specs=[pl.BlockSpec(memory_space=pl.ANY), pl.BlockSpec(memory_space=pl.ANY)],
+        out_specs=pl.BlockSpec(memory_space=pl.ANY),
+        scratch_shapes=[pltpu.SemaphoreType.DMA((2,))],
+        out_shape=jax.ShapeDtypeStruct((rows + sub, kv), base_weight.dtype),
+    )(base_weight, delta_rows)
+
+
 def tile_partials(tile_rows, tile_cols, layer_input, grad_values):
     tokens = layer_input.shape[0]
     listed = tile_rows.shape[0]
@@ -109,7 +130,7 @@
 
     sub = TILE * TILE // kv
     delta_rows = tile_delta.reshape(col_tiles, sub, TILE).transpose(1, 0, 2).reshape(sub, kv)
-    packed = jnp.concatenate([base_weight, delta_rows], axis=0)
+    packed = packed_shard(base_weight, delta_rows)
     gathered = lax.all_gather(packed, DP, axis=0, tiled=False)
 
     all_ids = lax.all_to_all(jnp.broadcast_to(tile_ids, (n,)), DP, 0, 0, tiled=True)

time: 133 us -> 165 us (1.24)
  Pallas kernels: 23.3 us -> 57.2 us
  other arithmetic: 5.76 us -> 3.48 us
    pallas_call x0 -> x1, Pallas kernels: none -> 33.9 us  [packed_shard(): pl.pallas_call(kernel, in_specs=[pl.BlockSpec(memory_space=pl.ANY), pl.Bl...]
    concatenate x1 -> x0, other arithmetic: 2.28 us -> none  [body(): packed = jnp.concatenate([base_weight, delta_rows], axis=0)]
  transfers between devices with their start and end apart: 4 -> 4, of which waited for: 4 -> 4; matrix products, arithmetic and copies ran while one was open for 3% -> 3% of each run, Pallas kernels for 18% -> 14%
where the time goes in v8:
time: 165 us; the launch traced here: 164 us
  waiting for transfers between devices  73.4 us (44%)
  Pallas kernels  57.2 us (35%)
  between operations  14.7 us (9%)
  starting transfers between devices  12.1 us (7%)
  other arithmetic  3.48 us (2%)
  local copies, waits for them, and re-layouts  3.15 us (2%)
    all_gather x1, waiting for transfers between devices, body(): gathered = lax.all_gather(packed, DP, axis=0, tiled=False)  62.4 us
    pallas_call x1, Pallas kernels, packed_shard(): pl.pallas_call(kernel, in_specs=[pl.BlockSpec(memory_space=pl.ANY), pl.Bl...  33.9 us
    pallas_call x1, Pallas kernels, merged_matmul(): pl.pallas_call(kernel, grid_spec=pltpu.PrefetchScalarGridSpec(num_scalar_...  12.5 us
    pallas_call x1, Pallas kernels, tile_partials(): pl.pallas_call(kernel, grid_spec=pltpu.PrefetchScalarGridSpec(num_scalar_...  10.8 us
    all_to_all x1, starting transfers between devices, body(): lax.all_to_all(jnp.broadcast_to(tile_ids, (n,)), DP, 0, 0, tiled=True)  7.41 us
    all_to_all x1, waiting for transfers between devices, body(): lax.all_to_all(jnp.broadcast_to(tile_ids, (n,)), DP, 0, 0, tiled=True)  6.36 us
    all_to_all x1, starting transfers between devices, body(): from_chips = lax.all_to_all(chip_sum, 'chips', 0, 0, tiled=True)  4.57 us
  transfers between devices with their start and end apart: 4, of which 4 were waited for; matrix products, arithmetic and copies ran while one was open for 3% of the time, Pallas kernels for 14%

profile of v8, /device:TPU:0, one launch (start us, length us, event | category | flops | bytes accessed | tf_op | source)
XLA Modules:
  0.0 164.0 jit_solution(905659618475340431)
XLA Ops:
  7.2 0.0 all-gather.3.cloned.1.call-start
  7.2 0.8 copy.9
  8.0 0.6 copy.12
  8.6 33.9 %shard_map.68 = bf16[528,1024]{1,0:T(8,128)(2,1)} custom-call(bf16[512,1024]{1,0:T(8,128)(2,1)} %b_ref.1, bf16[16,1024]{1,0:T(8,128)(2,1)} %bitcast.20), custom_call_target="tpu_custom_call" | custom-call | tf_op jit(solution)/shard_map/pallas_call | solution.py:88
  42.5 0.0 all-gather.3.cloned.1.call-update
  43.2 0.6 broadcast_in_dim.9
  43.8 7.4 %all-to-all-start = ((s32[16,1,1]{2,1,0:T(1,128)}), s32[16,1,1]{2,1,0:T(1,128)S(1)}, u32[]{:S(2)}, u32[]{:S(2)}) async-start(s32[16,1,1]{2,1,0:T(1,128)} %broadcast_in_dim.9), calls=%async_computation | async-start | bytes 16384 | tf_op jit(solution)/shard_map/all_to_all | solution.py:136
  51.2 6.4 %all-to-all-done = s32[16,1,1]{2,1,0:T(1,128)S(1)} async-done(((s32[16,1,1]{2,1,0:T(1,128)}), s32[16,1,1]{2,1,0:T(1,128)S(1)}, u32[]{:S(2)}, u32[]{:S(2)}) %all-to-all-start) | async-done | bytes 96 | tf_op jit(solution)/shard_map/all_to_all | solution.py:136
  57.5 0.4 reduce
  57.9 0.5 and_select_fusion
  58.5 10.8 %shard_map.69 = f32[16,128,128]{2,1,0:T(8,128)} custom-call(s32[16]{0:T(128)} %get-tuple-element.7.rows_ref, s32[16]{0:T(128)} %get-tuple-element.6.cols_ref, bf16[256,8192]{1,0:T(8,128)(2,1)} %x_ref.1, bf16[256,1024]{1,0:T(8,128)(2,1)} %gv_ref.1), custom_call_target="tpu_custom_call" | custom-call | tf_op jit(solution)/shard_map/pallas_call | solution.py:106
  69.3 1.2 dynamic-slice_bitcast_fusion
  70.5 0.1 collective-permute-start
  70.6 2.2 %collective-permute-done = f32[8,128,128]{2,1,0:T(8,128)S(1)} collective-permute-done((f32[8,128,128]{2,1,0:T(8,128)S(1)}, f32[8,128,128]{2,1,0:T(8,128)S(1)}, u32[]{:S(2)}, u32[]{:S(2)}) %collective-permute-start) | collective-permute-done | bytes 524320 | tf_op jit(solution)/shard_map/ppermute | solution.py:145
  72.7 1.9 %bitcast_add_fusion = f32[8,128,128]{2,1,0:T(8,128)} fusion(f32[8,128,128]{2,1,0:T(8,128)S(1)} %collective-permute-done, f32[8,2,128,128]{3,2,1,0:T(8,128)} %bitcast.19, s32[]{:T(128)S(6)} %select_n.21), kind=kLoop, calls=%fused_computation | loop fusion | flops 131072 | bytes 1572868 | tf_op jit(solution)/shard_map/add | solution.py:145
  74.6 62.4 %all-gather.3.cloned.1.call-done = bf16[8448,1024]{1,0:T(8,128)(2,1)} async-done(((bf16[528,1024]{1,0:T(8,128)(2,1)}), bf16[8448,1024]{1,0:T(8,128)(2,1)}) %all-gather.3.cloned.1.call-update) | async-done | bytes 17301520 | tf_op jit(solution)/shard_map/all_gather | solution.py:134
  137.0 4.6 %all-to-all-start.1 = ((f32[8,128,128]{2,1,0:T(8,128)}), f32[8,128,128]{2,1,0:T(8,128)S(1)}, u32[]{:S(2)}, u32[]{:S(2)}) async-start(f32[8,128,128]{2,1,0:T(8,128)} %bitcast_add_fusion), calls=%async_computation.1 | async-start | bytes 1048576 | tf_op jit(solution)/shard_map/all_to_all | solution.py:147
  141.6 12.5 %shard_map.70 = bf16[256,8192]{1,0:T(8,128)(2,1)} custom-call(s32[16]{0:T(128)} %get-tuple-element.7.rows_ref, s32[16]{0:T(128)} %get-tuple-element.6.cols_ref, bf16[256,1024]{1,0:T(8,128)(2,1)} %gv_ref.1, bf16[16,528,1024]{2,1,0:T(8,128)(2,1)} %bitcast.16, bf16[16,528,1024]{2,1,0:T(8,128)(2,1)} %bitcast.17), custom_call_target="tpu_custom_call" | custom-call | tf_op jit(solution)/shard_map/pallas_call | solution.py:59
  154.0 2.4 %all-to-all-done.1 = f32[8,128,128]{2,1,0:T(8,128)S(1)} async-done(((f32[8,128,128]{2,1,0:T(8,128)}), f32[8,128,128]{2,1,0:T(8,128)S(1)}, u32[]{:S(2)}, u32[]{:S(2)}) %all-to-all-start.1) | async-done | bytes 524320 | tf_op jit(solution)/shard_map/all_to_all | solution.py:147
  156.5 0.6 multiply_bitcast_fusion
  (1 shorter events, 0.0 us)
Async XLA Ops:
  7.2 129.8 %all-gather.3.cloned.1.call-start = ((), (), s32[]{:S(2)}) async-start(), calls=%async_computation.2 | async-start | bytes 18382848 | tf_op jit(solution)/shard_map/all_gather | solution.py:134
  43.8 13.8 %all-to-all-start = ((s32[16,1,1]{2,1,0:T(1,128)}), s32[16,1,1]{2,1,0:T(1,128)S(1)}, u32[]{:S(2)}, u32[]{:S(2)}) async-start(s32[16,1,1]{2,1,0:T(1,128)} %broadcast_in_dim.9), calls=%async_computation | async-start | bytes 16384 | tf_op jit(solution)/shard_map/all_to_all | solution.py:136
  70.5 2.3 %collective-permute-start = (f32[8,128,128]{2,1,0:T(8,128)S(1)}, f32[8,128,128]{2,1,0:T(8,128)S(1)}, u32[]{:S(2)}, u32[]{:S(2)}) collective-permute-start(f32[8,128,128]{2,1,0:T(8,128)S(1)} %dynamic-slice_bitcast_fusion), channel_id=1, source_target_pairs={{0,1},{1,0},{2,3},{3,2},{4,5},{5,4},{6,7},{7,6},{8,9},{9,8},{10,11... | collective-permute-start | bytes 1572872 | tf_op jit(solution)/shard_map/ppermute | solution.py:145
  137.0 19.5 %all-to-all-start.1 = ((f32[8,128,128]{2,1,0:T(8,128)}), f32[8,128,128]{2,1,0:T(8,128)S(1)}, u32[]{:S(2)}, u32[]{:S(2)}) async-start(f32[8,128,128]{2,1,0:T(8,128)} %bitcast_add_fusion), calls=%async_computation.1 | async-start | bytes 1048576 | tf_op jit(solution)/shard_map/all_to_all | solution.py:147
Sparse Core Ops, SparseCore 0:
  42.6 94.3 all-gather.2

commit v9 on v7

--- a/solution.py
+++ b/solution.py
@@ -9,67 +9,97 @@
 from jax.sharding import PartitionSpec as P
 
 TILE = 128
-BLOCK_ROWS = 4096
+CHUNK_ROWS = 512
 DP = ("chips", "core")
 
 
-def merged_matmul(tile_rows, tile_cols, grad_values, gathered, shard, interpret=False):
+def merged_matmul(tile_rows, tile_cols, grad_values, gathered, shard):
     tokens, kv = grad_values.shape
     n, packed_rows, _ = gathered.shape
     sub = packed_rows - shard
     d_model = n * shard
     col_tiles = kv // TILE
-    block_rows = max(min(BLOCK_ROWS, d_model), shard)
-    per_block = block_rows // shard
-    tiles_per_block = block_rows // TILE
+    chunk_rows = max(CHUNK_ROWS, shard)
+    per_chunk = chunk_rows // shard
+    chunks = d_model // chunk_rows
+    tiles_per_chunk = chunk_rows // TILE
 
-    def kernel(rows_ref, cols_ref, gv_ref, base_ref, delta_ref, out_ref):
-        i = pl.program_id(0)
+    def kernel(rows_ref, cols_ref, gv_ref, delta_ref, g_hbm, out_hbm, buf, obuf, in_sem, out_sem):
+        copies_in = [
+            pltpu.make_async_copy(
+                g_hbm.at[pl.ds(q * per_chunk, per_chunk), pl.ds(0, shard)],
+                buf.at[q],
+                in_sem.at[q],
+            )
+            for q in range(chunks)
+        ]
+        for cp in copies_in:
+            cp.start()
+        copies_out = []
+        for q in range(chunks):
+            copies_in[q].wait()
 
-        def patch(j, carry):
-            r = rows_ref[j] - i * tiles_per_block
+            def patch(j, carry):
+                r = rows_ref[j] - q * tiles_per_chunk
 
-            @pl.when((r >= 0) & (r < tiles_per_block))
-            def _():
-                c = cols_ref[j]
-                for cc in range(col_tiles):
+                @pl.when((r >= 0) & (r < tiles_per_chunk))
+                def _():
+                    c = cols_ref[j]
+                    for cc in range(col_tiles):
 
-                    @pl.when(c == cc)
-                    def _():
-                        cs = slice(cc * TILE, (cc + 1) * TILE)
-                        for a in range(col_tiles):
-                            at = r * TILE + a * sub
-                            si = at // shard
-                            rs = pl.ds(pl.multiple_of(at % shard, sub), sub)
-                            add = delta_ref[j, :, a * TILE:(a + 1) * TILE].astype(jnp.float32)
-                            cur = base_ref[si, rs, cs].astype(jnp.float32)
-                            base_ref[si, rs, cs] = (cur + add).astype(jnp.bfloat16)
+                        @pl.when(c == cc)
+                        def _():
+                            cs = slice(cc * TILE, (cc + 1) * TILE)
+                            for a in range(col_tiles):
+                                at = r * TILE + a * sub
+                                si = at // shard
+                                rs = pl.ds(pl.multiple_of(at % shard, sub), sub)
+                                add = delta_ref[j, :, a * TILE:(a + 1) * TILE].astype(jnp.float32)
+                                cur = buf[q, si, rs, cs].astype(jnp.float32)
+                                buf[q, si, rs, cs] = (cur + add).astype(jnp.bfloat16)
 
-            return carry
+                return carry
 
-        lax.fori_loop(0, n, patch, 0)
-        merged = base_ref[...].reshape(block_rows, kv)
-        out_ref[...] = lax.dot_general(
-            gv_ref[...],
-            merged,
-            (((1,), (1,)), ((), ())),
-            preferred_element_type=jnp.float32,
-        ).astype(out_ref.dtype)
+            lax.fori_loop(0, n, patch, 0)
+            slot = q % 2
+            if q >= 2:
+                copies_out[q - 2].wait()
+            obuf[slot] = lax.dot_general(
+                gv_ref[...],
+                buf[q].reshape(chunk_rows, kv),
+                (((1,), (1,)), ((), ())),
+                preferred_element_type=jnp.float32,
+            ).astype(obuf.dtype)
+            cp = pltpu.make_async_copy(
+                obuf.at[slot],
+                out_hbm.at[:, pl.ds(q * chunk_rows, chunk_rows)],
+                out_sem.at[slot],
+            )
+            cp.start()
+            copies_out.append(cp)
+        for cp in copies_out[-2:]:
+            cp.wait()
 
     return pl.pallas_call(
         kernel,
         grid_spec=pltpu.PrefetchScalarGridSpec(
             num_scalar_prefetch=2,
-            grid=(d_model // block_rows,),
+            grid=(1,),
             in_specs=[
                 pl.BlockSpec((tokens, kv), lambda i, r, c: (0, 0)),
-                pl.BlockSpec((per_block, shard, kv), lambda i, r, c: (i, 0, 0)),
                 pl.BlockSpec((n, sub, kv), lambda i, r, c: (0, shard // sub, 0)),
+                pl.BlockSpec(memory_space=pl.ANY),
             ],
-            out_specs=pl.BlockSpec((tokens, block_rows), lambda i, r, c: (0, i)),
+            out_specs=pl.BlockSpec(memory_space=pl.ANY),
+            scratch_shapes=[
+                pltpu.VMEM((chunks, per_chunk, shard, kv), jnp.bfloat16),
+                pltpu.VMEM((2, tokens, chunk_rows), jnp.bfloat16),
+                pltpu.SemaphoreType.DMA((chunks,)),
+                pltpu.SemaphoreType.DMA((2,)),
+            ],
         ),
         out_shape=jax.ShapeDtypeStruct((tokens, d_model), jnp.bfloat16),
-        interpret=interpret,
+        compiler_params=pltpu.CompilerParams(vmem_limit_bytes=56 * 1024 * 1024),
     )(tile_rows, tile_cols, grad_values, gathered, gathered)
 
 

time: 133 us -> 135 us (1.015)
  Pallas kernels: 23.3 us -> 27.6 us
  waiting for transfers between devices: 73.4 us -> 70.9 us
    pallas_call x1, Pallas kernels: 12.4 us -> 16.8 us  [merged_matmul(): pl.pallas_call(kernel, grid_spec=pltpu.PrefetchScalarGridSpec(num_scalar_...]
    all_to_all x1, waiting for transfers between devices: 2.45 us -> 0.01 us  [body(): from_chips = lax.all_to_all(chip_sum, 'chips', 0, 0, tiled=True)]
  transfers between devices with their start and end apart: 4 -> 4, of which waited for: 4 -> 3; matrix products, arithmetic and copies ran while one was open for 3% -> 3% of each run, Pallas kernels for 18% -> 21%
where the time goes in v9:
time: 135 us; the launch traced here: 134 us
  waiting for transfers between devices  70.9 us (53%)
  Pallas kernels  27.6 us (20%)
  between operations  14.7 us (11%)
  starting transfers between devices  12.1 us (9%)
  other arithmetic  5.76 us (4%)
  local copies, waits for them, and re-layouts  2.51 us (2%)
    all_gather x1, waiting for transfers between devices, body(): gathered = lax.all_gather(packed, DP, axis=0, tiled=False)  62.3 us
    pallas_call x1, Pallas kernels, merged_matmul(): pl.pallas_call(kernel, grid_spec=pltpu.PrefetchScalarGridSpec(num_scalar_...  16.8 us
    pallas_call x1, Pallas kernels, tile_partials(): pl.pallas_call(kernel, grid_spec=pltpu.PrefetchScalarGridSpec(num_scalar_...  10.9 us
    all_to_all x1, starting transfers between devices, body(): lax.all_to_all(jnp.broadcast_to(tile_ids, (n,)), DP, 0, 0, tiled=True)  7.41 us
    all_to_all x1, waiting for transfers between devices, body(): lax.all_to_all(jnp.broadcast_to(tile_ids, (n,)), DP, 0, 0, tiled=True)  6.36 us
    all_to_all x1, starting transfers between devices, body(): from_chips = lax.all_to_all(chip_sum, 'chips', 0, 0, tiled=True)  4.57 us
  transfers between devices with their start and end apart: 4, of which 3 were waited for; matrix products, arithmetic and copies ran while one was open for 3% of the time, Pallas kernels for 21%

profile of v9, /device:TPU:0, one launch (start us, length us, event | category | flops | bytes accessed | tf_op | source)
XLA Modules:
  0.0 133.7 jit_solution(16410622313440313624)
XLA Ops:
  7.2 0.0 all-gather.3.cloned.1.call-start
  7.2 0.8 copy.12
  8.0 2.3 %pad_maximum_fusion = bf16[528,1024]{1,0:T(8,128)(2,1)} fusion(bf16[16,1024]{1,0:T(8,128)(2,1)S(1)} %bitcast.21, bf16[512,1024]{1,0:T(8,128)(2,1)} %param.7), kind=kLoop, calls=%fused_computation | loop fusion | flops 2162688 | bytes 2162688 | tf_op jit(solution)/shard_map/concatenate | solution.py:142
  10.2 0.0 all-gather.3.cloned.1.call-update
  10.9 0.6 broadcast_in_dim.9
  11.5 7.4 %all-to-all-start = ((s32[16,1,1]{2,1,0:T(1,128)}), s32[16,1,1]{2,1,0:T(1,128)S(1)}, u32[]{:S(2)}, u32[]{:S(2)}) async-start(s32[16,1,1]{2,1,0:T(1,128)} %broadcast_in_dim.9), calls=%async_computation | async-start | bytes 16384 | tf_op jit(solution)/shard_map/all_to_all | solution.py:145
  19.0 6.4 %all-to-all-done = s32[16,1,1]{2,1,0:T(1,128)S(1)} async-done(((s32[16,1,1]{2,1,0:T(1,128)}), s32[16,1,1]{2,1,0:T(1,128)S(1)}, u32[]{:S(2)}, u32[]{:S(2)}) %all-to-all-start) | async-done | bytes 96 | tf_op jit(solution)/shard_map/all_to_all | solution.py:145
  25.3 0.4 reduce
  25.7 0.5 and_select_fusion
  26.2 10.9 %shard_map.68 = f32[16,128,128]{2,1,0:T(8,128)} custom-call(s32[16]{0:T(128)} %get-tuple-element.7.rows_ref, s32[16]{0:T(128)} %get-tuple-element.6.cols_ref, bf16[256,8192]{1,0:T(8,128)(2,1)} %x_ref.1, bf16[256,1024]{1,0:T(8,128)(2,1)} %gv_ref.1), custom_call_target="tpu_custom_call" | custom-call | tf_op jit(solution)/shard_map/pallas_call | solution.py:115
  37.1 1.1 dynamic-slice_bitcast_fusion
  38.3 0.1 collective-permute-start
  38.3 2.2 %collective-permute-done = f32[8,128,128]{2,1,0:T(8,128)S(1)} collective-permute-done((f32[8,128,128]{2,1,0:T(8,128)S(1)}, f32[8,128,128]{2,1,0:T(8,128)S(1)}, u32[]{:S(2)}, u32[]{:S(2)}) %collective-permute-start) | collective-permute-done | bytes 524320 | tf_op jit(solution)/shard_map/ppermute | solution.py:154
  40.5 1.9 %bitcast_add_fusion = f32[8,128,128]{2,1,0:T(8,128)} fusion(f32[8,128,128]{2,1,0:T(8,128)S(1)} %collective-permute-done, f32[8,2,128,128]{3,2,1,0:T(8,128)} %bitcast.20, s32[]{:T(128)S(6)} %select_n.21), kind=kLoop, calls=%fused_computation.1 | loop fusion | flops 131072 | bytes 1572868 | tf_op jit(solution)/shard_map/add | solution.py:154
  42.4 62.3 %all-gather.3.cloned.1.call-done = bf16[8448,1024]{1,0:T(8,128)(2,1)} async-done(((bf16[528,1024]{1,0:T(8,128)(2,1)}), bf16[8448,1024]{1,0:T(8,128)(2,1)}) %all-gather.3.cloned.1.call-update) | async-done | bytes 17301520 | tf_op jit(solution)/shard_map/all_gather | solution.py:143
  104.8 4.6 %all-to-all-start.1 = ((f32[8,128,128]{2,1,0:T(8,128)}), f32[8,128,128]{2,1,0:T(8,128)S(1)}, u32[]{:S(2)}, u32[]{:S(2)}) async-start(f32[8,128,128]{2,1,0:T(8,128)} %bitcast_add_fusion), calls=%async_computation.1 | async-start | bytes 1048576 | tf_op jit(solution)/shard_map/all_to_all | solution.py:156
  109.3 16.8 %shard_map.69 = bf16[256,8192]{1,0:T(8,128)(2,1)} custom-call(s32[16]{0:T(128)} %get-tuple-element.7.rows_ref, s32[16]{0:T(128)} %get-tuple-element.6.cols_ref, bf16[256,1024]{1,0:T(8,128)(2,1)} %gv_ref.1, bf16[16,528,1024]{2,1,0:T(8,128)(2,1)} %bitcast.17, bf16[16,528,1024]{2,1,0:T(8,128)(2,1)} %bitcast.18), custom_call_target="tpu_custom_call" | custom-call | tf_op jit(solution)/shard_map/pallas_call | solution.py:83
  126.1 0.0 all-to-all-done.1
  126.2 0.6 multiply_bitcast_fusion
  (1 shorter events, 0.0 us)
Async XLA Ops:
  7.2 97.6 %all-gather.3.cloned.1.call-start = ((), (), s32[]{:S(2)}) async-start(), calls=%async_computation.2 | async-start | bytes 18382848 | tf_op jit(solution)/shard_map/all_gather | solution.py:143
  11.5 13.8 %all-to-all-start = ((s32[16,1,1]{2,1,0:T(1,128)}), s32[16,1,1]{2,1,0:T(1,128)S(1)}, u32[]{:S(2)}, u32[]{:S(2)}) async-start(s32[16,1,1]{2,1,0:T(1,128)} %broadcast_in_dim.9), calls=%async_computation | async-start | bytes 16384 | tf_op jit(solution)/shard_map/all_to_all | solution.py:145
  38.3 2.3 %collective-permute-start = (f32[8,128,128]{2,1,0:T(8,128)S(1)}, f32[8,128,128]{2,1,0:T(8,128)S(1)}, u32[]{:S(2)}, u32[]{:S(2)}) collective-permute-start(f32[8,128,128]{2,1,0:T(8,128)S(1)} %dynamic-slice_bitcast_fusion), channel_id=1, source_target_pairs={{0,1},{1,0},{2,3},{3,2},{4,5},{5,4},{6,7},{7,6},{8,9},{9,8},{10,11... | collective-permute-start | bytes 1572872 | tf_op jit(solution)/shard_map/ppermute | solution.py:154
  104.8 21.4 %all-to-all-start.1 = ((f32[8,128,128]{2,1,0:T(8,128)}), f32[8,128,128]{2,1,0:T(8,128)S(1)}, u32[]{:S(2)}, u32[]{:S(2)}) async-start(f32[8,128,128]{2,1,0:T(8,128)} %bitcast_add_fusion), calls=%async_computation.1 | async-start | bytes 1048576 | tf_op jit(solution)/shard_map/all_to_all | solution.py:156
Sparse Core Ops, SparseCore 0:
  10.4 94.3 all-gather.2

commit v10 on v7

--- a/solution.py
+++ b/solution.py
@@ -31,19 +31,14 @@
 
             @pl.when((r >= 0) & (r < tiles_per_block))
             def _():
-                c = cols_ref[j]
-                for cc in range(col_tiles):
-
-                    @pl.when(c == cc)
-                    def _():
-                        cs = slice(cc * TILE, (cc + 1) * TILE)
-                        for a in range(col_tiles):
-                            at = r * TILE + a * sub
-                            si = at // shard
-                            rs = pl.ds(pl.multiple_of(at % shard, sub), sub)
-                            add = delta_ref[j, :, a * TILE:(a + 1) * TILE].astype(jnp.float32)
-                            cur = base_ref[si, rs, cs].astype(jnp.float32)
-                            base_ref[si, rs, cs] = (cur + add).astype(jnp.bfloat16)
+                cs = pl.ds(pl.multiple_of(cols_ref[j] * TILE, TILE), TILE)
+                for a in range(col_tiles):
+                    at = r * TILE + a * sub
+                    si = at // shard
+                    rs = pl.ds(pl.multiple_of(at % shard, sub), sub)
+                    add = delta_ref[j, :, a * TILE:(a + 1) * TILE].astype(jnp.float32)
+                    cur = base_ref[si, rs, cs].astype(jnp.float32)
+                    base_ref[si, rs, cs] = (cur + add).astype(jnp.bfloat16)
 
             return carry
 

time: 133 us -> 133 us (level)
  transfers between devices with their start and end apart: 4 -> 4, of which waited for: 4 -> 4; matrix products, arithmetic and copies ran while one was open for 3% -> 3% of each run, Pallas kernels for 18% -> 17%
where the time goes in v10:
time: 133 us; the launch traced here: 132 us
  waiting for transfers between devices  74.2 us (56%)
  Pallas kernels  22.5 us (17%)
  between operations  14.7 us (11%)
  starting transfers between devices  12.1 us (9%)
  other arithmetic  5.76 us (4%)
  local copies, waits for them, and re-layouts  2.54 us (2%)
    all_gather x1, waiting for transfers between devices, body(): gathered = lax.all_gather(packed, DP, axis=0, tiled=False)  62.4 us
    pallas_call x1, Pallas kernels, merged_matmul(): pl.pallas_call(kernel, grid_spec=pltpu.PrefetchScalarGridSpec(num_scalar_...  11.7 us
    pallas_call x1, Pallas kernels, tile_partials(): pl.pallas_call(kernel, grid_spec=pltpu.PrefetchScalarGridSpec(num_scalar_...  10.8 us
    all_to_all x1, starting transfers between devices, body(): lax.all_to_all(jnp.broadcast_to(tile_ids, (n,)), DP, 0, 0, tiled=True)  7.41 us
    all_to_all x1, waiting for transfers between devices, body(): lax.all_to_all(jnp.broadcast_to(tile_ids, (n,)), DP, 0, 0, tiled=True)  6.36 us
    all_to_all x1, starting transfers between devices, body(): from_chips = lax.all_to_all(chip_sum, 'chips', 0, 0, tiled=True)  4.57 us
    all_to_all x1, waiting for transfers between devices, body(): from_chips = lax.all_to_all(chip_sum, 'chips', 0, 0, tiled=True)  3.22 us
  transfers between devices with their start and end apart: 4, of which 4 were waited for; matrix products, arithmetic and copies ran while one was open for 3% of the time, Pallas kernels for 17%

profile of v10, /device:TPU:0, one launch (start us, length us, event | category | flops | bytes accessed | tf_op | source)
XLA Modules:
  0.0 131.8 jit_solution(5564113301518564600)
XLA Ops:
  7.2 0.0 all-gather.3.cloned.1.call-start
  7.2 0.8 copy.12
  8.0 2.3 %pad_maximum_fusion = bf16[528,1024]{1,0:T(8,128)(2,1)} fusion(bf16[16,1024]{1,0:T(8,128)(2,1)S(1)} %bitcast.21, bf16[512,1024]{1,0:T(8,128)(2,1)} %param.7), kind=kLoop, calls=%fused_computation | loop fusion | flops 2162688 | bytes 2162688 | tf_op jit(solution)/shard_map/concatenate | solution.py:107
  10.2 0.0 all-gather.3.cloned.1.call-update
  10.9 0.6 broadcast_in_dim.9
  11.5 7.4 %all-to-all-start = ((s32[16,1,1]{2,1,0:T(1,128)}), s32[16,1,1]{2,1,0:T(1,128)S(1)}, u32[]{:S(2)}, u32[]{:S(2)}) async-start(s32[16,1,1]{2,1,0:T(1,128)} %broadcast_in_dim.9), calls=%async_computation | async-start | bytes 16384 | tf_op jit(solution)/shard_map/all_to_all | solution.py:110
  19.0 6.4 %all-to-all-done = s32[16,1,1]{2,1,0:T(1,128)S(1)} async-done(((s32[16,1,1]{2,1,0:T(1,128)}), s32[16,1,1]{2,1,0:T(1,128)S(1)}, u32[]{:S(2)}, u32[]{:S(2)}) %all-to-all-start) | async-done | bytes 96 | tf_op jit(solution)/shard_map/all_to_all | solution.py:110
  25.3 0.4 reduce
  25.7 0.5 and_select_fusion
  26.2 10.8 %shard_map.68 = f32[16,128,128]{2,1,0:T(8,128)} custom-call(s32[16]{0:T(128)} %get-tuple-element.7.rows_ref, s32[16]{0:T(128)} %get-tuple-element.6.cols_ref, bf16[256,8192]{1,0:T(8,128)(2,1)} %x_ref.1, bf16[256,1024]{1,0:T(8,128)(2,1)} %gv_ref.1), custom_call_target="tpu_custom_call" | custom-call | tf_op jit(solution)/shard_map/pallas_call | solution.py:80
  37.1 1.2 dynamic-slice_bitcast_fusion
  38.2 0.1 collective-permute-start
  38.3 2.2 %collective-permute-done = f32[8,128,128]{2,1,0:T(8,128)S(1)} collective-permute-done((f32[8,128,128]{2,1,0:T(8,128)S(1)}, f32[8,128,128]{2,1,0:T(8,128)S(1)}, u32[]{:S(2)}, u32[]{:S(2)}) %collective-permute-start) | collective-permute-done | bytes 524320 | tf_op jit(solution)/shard_map/ppermute | solution.py:119
  40.5 1.9 %bitcast_add_fusion = f32[8,128,128]{2,1,0:T(8,128)} fusion(f32[8,128,128]{2,1,0:T(8,128)S(1)} %collective-permute-done, f32[8,2,128,128]{3,2,1,0:T(8,128)} %bitcast.20, s32[]{:T(128)S(6)} %select_n.21), kind=kLoop, calls=%fused_computation.1 | loop fusion | flops 131072 | bytes 1572868 | tf_op jit(solution)/shard_map/add | solution.py:119
  42.4 62.4 %all-gather.3.cloned.1.call-done = bf16[8448,1024]{1,0:T(8,128)(2,1)} async-done(((bf16[528,1024]{1,0:T(8,128)(2,1)}), bf16[8448,1024]{1,0:T(8,128)(2,1)}) %all-gather.3.cloned.1.call-update) | async-done | bytes 17301520 | tf_op jit(solution)/shard_map/all_gather | solution.py:108
  104.8 4.6 %all-to-all-start.1 = ((f32[8,128,128]{2,1,0:T(8,128)}), f32[8,128,128]{2,1,0:T(8,128)S(1)}, u32[]{:S(2)}, u32[]{:S(2)}) async-start(f32[8,128,128]{2,1,0:T(8,128)} %bitcast_add_fusion), calls=%async_computation.1 | async-start | bytes 1048576 | tf_op jit(solution)/shard_map/all_to_all | solution.py:121
  109.3 11.7 %shard_map.69 = bf16[256,8192]{1,0:T(8,128)(2,1)} custom-call(s32[16]{0:T(128)} %get-tuple-element.7.rows_ref, s32[16]{0:T(128)} %get-tuple-element.6.cols_ref, bf16[256,1024]{1,0:T(8,128)(2,1)} %gv_ref.1, bf16[16,528,1024]{2,1,0:T(8,128)(2,1)} %bitcast.17, bf16[16,528,1024]{2,1,0:T(8,128)(2,1)} %bitcast.18), custom_call_target="tpu_custom_call" | custom-call | tf_op jit(solution)/shard_map/pallas_call | solution.py:54
  121.0 3.2 %all-to-all-done.1 = f32[8,128,128]{2,1,0:T(8,128)S(1)} async-done(((f32[8,128,128]{2,1,0:T(8,128)}), f32[8,128,128]{2,1,0:T(8,128)S(1)}, u32[]{:S(2)}, u32[]{:S(2)}) %all-to-all-start.1) | async-done | bytes 524320 | tf_op jit(solution)/shard_map/all_to_all | solution.py:121
  124.3 0.6 multiply_bitcast_fusion
  (1 shorter events, 0.0 us)
Async XLA Ops:
  7.2 97.6 %all-gather.3.cloned.1.call-start = ((), (), s32[]{:S(2)}) async-start(), calls=%async_computation.2 | async-start | bytes 18382848 | tf_op jit(solution)/shard_map/all_gather | solution.py:108
  11.5 13.8 %all-to-all-start = ((s32[16,1,1]{2,1,0:T(1,128)}), s32[16,1,1]{2,1,0:T(1,128)S(1)}, u32[]{:S(2)}, u32[]{:S(2)}) async-start(s32[16,1,1]{2,1,0:T(1,128)} %broadcast_in_dim.9), calls=%async_computation | async-start | bytes 16384 | tf_op jit(solution)/shard_map/all_to_all | solution.py:110
  38.2 2.3 %collective-permute-start = (f32[8,128,128]{2,1,0:T(8,128)S(1)}, f32[8,128,128]{2,1,0:T(8,128)S(1)}, u32[]{:S(2)}, u32[]{:S(2)}) collective-permute-start(f32[8,128,128]{2,1,0:T(8,128)S(1)} %dynamic-slice_bitcast_fusion), channel_id=1, source_target_pairs={{0,1},{1,0},{2,3},{3,2},{4,5},{5,4},{6,7},{7,6},{8,9},{9,8},{10,11... | collective-permute-start | bytes 1572872 | tf_op jit(solution)/shard_map/ppermute | solution.py:119
  104.8 19.5 %all-to-all-start.1 = ((f32[8,128,128]{2,1,0:T(8,128)}), f32[8,128,128]{2,1,0:T(8,128)S(1)}, u32[]{:S(2)}, u32[]{:S(2)}) async-start(f32[8,128,128]{2,1,0:T(8,128)} %bitcast_add_fusion), calls=%async_computation.1 | async-start | bytes 1048576 | tf_op jit(solution)/shard_map/all_to_all | solution.py:121
Sparse Core Ops, SparseCore 0:
  10.4 94.3 all-gather.2

commit v11 on v10

--- a/solution.py
+++ b/solution.py
@@ -68,6 +68,22 @@
     )(tile_rows, tile_cols, grad_values, gathered, gathered)
 
 
+def packed_shard(base_weight, tile_delta):
+    rows, kv = base_weight.shape
+    col_tiles = kv // TILE
+    sub = TILE * TILE // kv
+
+    def kernel(b_ref, d_ref, o_ref):
+        o_ref[:rows, :] = b_ref[...]
+        for a in range(col_tiles):
+            o_ref[rows:, a * TILE:(a + 1) * TILE] = d_ref[0, a * sub:(a + 1) * sub, :]
+
+    return pl.pallas_call(
+        kernel,
+        out_shape=jax.ShapeDtypeStruct((rows + sub, kv), base_weight.dtype),
+    )(base_weight, tile_delta)
+
+
 def tile_partials(tile_rows, tile_cols, layer_input, grad_values):
     tokens = layer_input.shape[0]
     listed = tile_rows.shape[0]
@@ -102,9 +118,7 @@
     row_tiles = d_model // TILE
     col_tiles = kv // TILE
 
-    sub = TILE * TILE // kv
-    delta_rows = tile_delta.reshape(col_tiles, sub, TILE).transpose(1, 0, 2).reshape(sub, kv)
-    packed = jnp.concatenate([base_weight, delta_rows], axis=0)
+    packed = packed_shard(base_weight, tile_delta)
     gathered = lax.all_gather(packed, DP, axis=0, tiled=False)
 
     all_ids = lax.all_to_all(jnp.broadcast_to(tile_ids, (n,)), DP, 0, 0, tiled=True)

time: 133 us -> 132 us (level)
  Pallas kernels: 22.5 us -> 24.8 us
  other arithmetic: 5.76 us -> 3.47 us
    pallas_call x0 -> x1, Pallas kernels: none -> 2.28 us  [packed_shard(): pl.pallas_call(kernel, out_shape=jax.ShapeDtypeStruct((rows + sub, kv), b...]
    concatenate x1 -> x0, other arithmetic: 2.28 us -> none  [body(): packed = jnp.concatenate([base_weight, delta_rows], axis=0)]
where the time goes in v11:
time: 132 us; the launch traced here: 131 us
  waiting for transfers between devices  74.8 us (57%)
  Pallas kernels  24.8 us (19%)
  between operations  14.7 us (11%)
  starting transfers between devices  12.1 us (9%)
  other arithmetic  3.47 us (3%)
  local copies, waits for them, and re-layouts  1.68 us (1%)
    all_gather x1, waiting for transfers between devices, body(): gathered = lax.all_gather(packed, DP, axis=0, tiled=False)  63.3 us
    pallas_call x1, Pallas kernels, merged_matmul(): pl.pallas_call(kernel, grid_spec=pltpu.PrefetchScalarGridSpec(num_scalar_...  11.7 us
    pallas_call x1, Pallas kernels, tile_partials(): pl.pallas_call(kernel, grid_spec=pltpu.PrefetchScalarGridSpec(num_scalar_...  10.8 us
    all_to_all x1, starting transfers between devices, body(): lax.all_to_all(jnp.broadcast_to(tile_ids, (n,)), DP, 0, 0, tiled=True)  7.41 us
    all_to_all x1, waiting for transfers between devices, body(): lax.all_to_all(jnp.broadcast_to(tile_ids, (n,)), DP, 0, 0, tiled=True)  6.36 us
    all_to_all x1, starting transfers between devices, body(): from_chips = lax.all_to_all(chip_sum, 'chips', 0, 0, tiled=True)  4.53 us
    all_to_all x1, waiting for transfers between devices, body(): from_chips = lax.all_to_all(chip_sum, 'chips', 0, 0, tiled=True)  3.2 us
  transfers between devices with their start and end apart: 4, of which 4 were waited for; matrix products, arithmetic and copies ran while one was open for 3% of the time, Pallas kernels for 17%

profile of v11, /device:TPU:0, one launch (start us, length us, event | category | flops | bytes accessed | tf_op | source)
XLA Modules:
  0.0 131.4 jit_solution(7367264196227237601)
XLA Ops:
  7.2 0.0 all-gather.3.cloned.1.call-start
  7.2 2.3 %shard_map.68 = bf16[528,1024]{1,0:T(8,128)(2,1)} custom-call(bf16[512,1024]{1,0:T(8,128)(2,1)} %b_ref.1, bf16[1,128,128]{2,1,0:T(8,128)(2,1)} %d_ref.1), custom_call_target="tpu_custom_call" | custom-call | tf_op jit(solution)/shard_map/pallas_call | solution.py:81
  9.5 0.0 all-gather.3.cloned.1.call-update
  10.2 0.6 broadcast_in_dim.9
  10.8 7.4 %all-to-all-start = ((s32[16,1,1]{2,1,0:T(1,128)}), s32[16,1,1]{2,1,0:T(1,128)S(1)}, u32[]{:S(2)}, u32[]{:S(2)}) async-start(s32[16,1,1]{2,1,0:T(1,128)} %broadcast_in_dim.9), calls=%async_computation | async-start | bytes 16384 | tf_op jit(solution)/shard_map/all_to_all | solution.py:124
  18.2 6.4 %all-to-all-done = s32[16,1,1]{2,1,0:T(1,128)S(1)} async-done(((s32[16,1,1]{2,1,0:T(1,128)}), s32[16,1,1]{2,1,0:T(1,128)S(1)}, u32[]{:S(2)}, u32[]{:S(2)}) %all-to-all-start) | async-done | bytes 96 | tf_op jit(solution)/shard_map/all_to_all | solution.py:124
  24.6 0.4 reduce
  24.9 0.5 and_select_fusion
  25.5 10.8 %shard_map.69 = f32[16,128,128]{2,1,0:T(8,128)} custom-call(s32[16]{0:T(128)} %get-tuple-element.7.rows_ref, s32[16]{0:T(128)} %get-tuple-element.6.cols_ref, bf16[256,8192]{1,0:T(8,128)(2,1)} %x_ref.1, bf16[256,1024]{1,0:T(8,128)(2,1)} %gv_ref.1), custom_call_target="tpu_custom_call" | custom-call | tf_op jit(solution)/shard_map/pallas_call | solution.py:96
  36.3 1.1 dynamic-slice_bitcast_fusion
  37.4 0.1 collective-permute-start
  37.4 1.9 %collective-permute-done = f32[8,128,128]{2,1,0:T(8,128)S(1)} collective-permute-done((f32[8,128,128]{2,1,0:T(8,128)S(1)}, f32[8,128,128]{2,1,0:T(8,128)S(1)}, u32[]{:S(2)}, u32[]{:S(2)}) %collective-permute-start) | collective-permute-done | bytes 524320 | tf_op jit(solution)/shard_map/ppermute | solution.py:133
  39.3 1.9 %bitcast_add_fusion = f32[8,128,128]{2,1,0:T(8,128)} fusion(f32[8,128,128]{2,1,0:T(8,128)S(1)} %collective-permute-done, f32[8,2,128,128]{3,2,1,0:T(8,128)} %bitcast.13, s32[]{:T(128)S(6)} %select_n.21), kind=kLoop, calls=%fused_computation | loop fusion | flops 131072 | bytes 1572868 | tf_op jit(solution)/shard_map/add | solution.py:133
  41.2 63.3 %all-gather.3.cloned.1.call-done = bf16[8448,1024]{1,0:T(8,128)(2,1)} async-done(((bf16[528,1024]{1,0:T(8,128)(2,1)}), bf16[8448,1024]{1,0:T(8,128)(2,1)}) %all-gather.3.cloned.1.call-update) | async-done | bytes 17301520 | tf_op jit(solution)/shard_map/all_gather | solution.py:122
  104.5 4.5 %all-to-all-start.1 = ((f32[8,128,128]{2,1,0:T(8,128)}), f32[8,128,128]{2,1,0:T(8,128)S(1)}, u32[]{:S(2)}, u32[]{:S(2)}) async-start(f32[8,128,128]{2,1,0:T(8,128)} %bitcast_add_fusion), calls=%async_computation.1 | async-start | bytes 1048576 | tf_op jit(solution)/shard_map/all_to_all | solution.py:135
  109.0 11.7 %shard_map.70 = bf16[256,8192]{1,0:T(8,128)(2,1)} custom-call(s32[16]{0:T(128)} %get-tuple-element.7.rows_ref, s32[16]{0:T(128)} %get-tuple-element.6.cols_ref, bf16[256,1024]{1,0:T(8,128)(2,1)} %gv_ref.1, bf16[16,528,1024]{2,1,0:T(8,128)(2,1)} %bitcast.10, bf16[16,528,1024]{2,1,0:T(8,128)(2,1)} %bitcast.11), custom_call_target="tpu_custom_call" | custom-call | tf_op jit(solution)/shard_map/pallas_call | solution.py:54
  120.7 3.2 %all-to-all-done.1 = f32[8,128,128]{2,1,0:T(8,128)S(1)} async-done(((f32[8,128,128]{2,1,0:T(8,128)}), f32[8,128,128]{2,1,0:T(8,128)S(1)}, u32[]{:S(2)}, u32[]{:S(2)}) %all-to-all-start.1) | async-done | bytes 524320 | tf_op jit(solution)/shard_map/all_to_all | solution.py:135
  124.0 0.6 multiply_bitcast_fusion
  (1 shorter events, 0.0 us)
Async XLA Ops:
  7.2 97.3 %all-gather.3.cloned.1.call-start = ((), (), s32[]{:S(2)}) async-start(), calls=%async_computation.2 | async-start | bytes 18382848 | tf_op jit(solution)/shard_map/all_gather | solution.py:122
  10.8 13.8 %all-to-all-start = ((s32[16,1,1]{2,1,0:T(1,128)}), s32[16,1,1]{2,1,0:T(1,128)S(1)}, u32[]{:S(2)}, u32[]{:S(2)}) async-start(s32[16,1,1]{2,1,0:T(1,128)} %broadcast_in_dim.9), calls=%async_computation | async-start | bytes 16384 | tf_op jit(solution)/shard_map/all_to_all | solution.py:124
  37.4 2.0 %collective-permute-start = (f32[8,128,128]{2,1,0:T(8,128)S(1)}, f32[8,128,128]{2,1,0:T(8,128)S(1)}, u32[]{:S(2)}, u32[]{:S(2)}) collective-permute-start(f32[8,128,128]{2,1,0:T(8,128)S(1)} %dynamic-slice_bitcast_fusion), channel_id=1, source_target_pairs={{0,1},{1,0},{2,3},{3,2},{4,5},{5,4},{6,7},{7,6},{8,9},{9,8},{10,11... | collective-permute-start | bytes 1572872 | tf_op jit(solution)/shard_map/ppermute | solution.py:133
  104.5 19.4 %all-to-all-start.1 = ((f32[8,128,128]{2,1,0:T(8,128)}), f32[8,128,128]{2,1,0:T(8,128)S(1)}, u32[]{:S(2)}, u32[]{:S(2)}) async-start(f32[8,128,128]{2,1,0:T(8,128)} %bitcast_add_fusion), calls=%async_computation.1 | async-start | bytes 1048576 | tf_op jit(solution)/shard_map/all_to_all | solution.py:135
Sparse Core Ops, SparseCore 0:
  10.1 94.3 all-gather.2

commit v12 on v11

--- a/solution.py
+++ b/solution.py
@@ -10,7 +10,7 @@
 
 TILE = 128
 BLOCK_ROWS = 4096
-DP = ("chips", "core")
+DP = ("za", "zb", "core")
 
 
 def merged_matmul(tile_rows, tile_cols, grad_values, gathered, shard, interpret=False):
@@ -109,7 +109,9 @@
 
 
 def body(layer_input, grad_values, base_weight, tile_ids, tile_delta):
-    chips = lax.axis_size("chips")
+    outer = lax.axis_size("za")
+    inner = lax.axis_size("zb")
+    chips = outer * inner
     n = 2 * chips
     tokens_here = layer_input.shape[0]
     d_model = layer_input.shape[1]
@@ -131,8 +133,17 @@
     mine = lax.dynamic_index_in_dim(partial, core, axis=1, keepdims=False)
     other = lax.dynamic_index_in_dim(partial, 1 - core, axis=1, keepdims=False)
     chip_sum = mine + lax.ppermute(other, "core", [(0, 1), (1, 0)])
+    if inner == 2:
+        pair = chip_sum.reshape(outer, inner, TILE, TILE)
+        at = lax.axis_index("zb")
+        keep = lax.dynamic_index_in_dim(pair, at, axis=1, keepdims=False)
+        give = lax.dynamic_index_in_dim(pair, 1 - at, axis=1, keepdims=False)
+        chip_sum = keep + lax.ppermute(give, "zb", [(0, 1), (1, 0)])
+        across = "za"
+    else:
+        across = ("za", "zb")
     gathered, chip_sum = lax.optimization_barrier((gathered, chip_sum))
-    from_chips = lax.all_to_all(chip_sum, "chips", 0, 0, tiled=True)
+    from_chips = lax.all_to_all(chip_sum, across, 0, 0, tiled=True)
     factor = 1.0 / math.sqrt(tokens_here * n)
     grad_tiles = jnp.sum(from_chips, axis=0, keepdims=True) * factor
 
@@ -142,7 +153,11 @@
 
 def solution(mesh):
     groups, dp = mesh.devices.shape
-    split = Mesh(mesh.devices.reshape(groups, dp // 2, 2), ("groups",) + DP)
+    seq = list(mesh.devices[0][::2])
+    changes = [sum(a.coords[i] != b.coords[i] for a, b in zip(seq, seq[1:])) for i in range(3)]
+    slowest = min((c, i) for i, c in enumerate(changes) if c > 0)[1]
+    inner = len(seq) // (changes[slowest] + 1)
+    split = Mesh(mesh.devices.reshape(groups, dp // 2 // inner, inner, 2), ("groups",) + DP)
     tokens = ("groups",) + DP
     placed = (
         P(tokens, None),

time: 132 us -> 135 us (1.023)
  waiting for transfers between devices: 74.8 us -> 76.3 us
    ppermute x0 -> x1, waiting for transfers between devices: none -> 14 us  [body(): chip_sum = keep + lax.ppermute(give, 'zb', [(0, 1), (1, 0)])]
    all_gather x1, waiting for transfers between devices: 63.3 us -> 54.1 us  [body(): gathered = lax.all_gather(packed, DP, axis=0, tiled=False)]
    all_to_all x1, waiting for transfers between devices: 3.2 us -> 0.01 us  [body(): from_chips = lax.all_to_all(chip_sum, across, 0, 0, tiled=True)]
  transfers between devices with their start and end apart: 4 -> 5, of which waited for: 4 -> 4; matrix products, arithmetic and copies ran while one was open for 3% -> 3% of each run, Pallas kernels for 17% -> 17%
where the time goes in v12:
time: 135 us; the launch traced here: 134 us
  waiting for transfers between devices  76.3 us (57%)
  Pallas kernels  24.9 us (18%)
  between operations  14.7 us (11%)
  starting transfers between devices  12.9 us (10%)
  other arithmetic  3.38 us (3%)
  local copies, waits for them, and re-layouts  1.71 us (1%)
    all_gather x1, waiting for transfers between devices, body(): gathered = lax.all_gather(packed, DP, axis=0, tiled=False)  54.1 us
    ppermute x1, waiting for transfers between devices, body(): chip_sum = keep + lax.ppermute(give, 'zb', [(0, 1), (1, 0)])  14 us
    pallas_call x1, Pallas kernels, merged_matmul(): pl.pallas_call(kernel, grid_spec=pltpu.PrefetchScalarGridSpec(num_scalar_...  11.8 us
    pallas_call x1, Pallas kernels, tile_partials(): pl.pallas_call(kernel, grid_spec=pltpu.PrefetchScalarGridSpec(num_scalar_...  10.8 us
    all_to_all x1, starting transfers between devices, body(): lax.all_to_all(jnp.broadcast_to(tile_ids, (n,)), DP, 0, 0, tiled=True)  7.41 us
    all_to_all x1, waiting for transfers between devices, body(): lax.all_to_all(jnp.broadcast_to(tile_ids, (n,)), DP, 0, 0, tiled=True)  6.36 us
    all_to_all x1, starting transfers between devices, body(): from_chips = lax.all_to_all(chip_sum, across, 0, 0, tiled=True)  4.74 us
  transfers between devices with their start and end apart: 5, of which 4 were waited for; matrix products, arithmetic and copies ran while one was open for 3% of the time, Pallas kernels for 17%

profile of v12, /device:TPU:0, one launch (start us, length us, event | category | flops | bytes accessed | tf_op | source)
XLA Modules:
  0.0 134.0 jit_solution(3855106852607140089)
XLA Ops:
  7.2 0.0 all-gather.3.cloned.1.call-start
  7.2 2.3 %shard_map.68 = bf16[528,1024]{1,0:T(8,128)(2,1)} custom-call(bf16[512,1024]{1,0:T(8,128)(2,1)} %b_ref.1, bf16[1,128,128]{2,1,0:T(8,128)(2,1)} %d_ref.1), custom_call_target="tpu_custom_call" | custom-call | tf_op jit(solution)/shard_map/pallas_call | solution.py:81
  9.5 0.0 all-gather.3.cloned.1.call-update
  10.2 0.6 broadcast_in_dim.9
  10.8 7.4 %all-to-all-start = ((s32[16,1,1]{2,1,0:T(1,128)}), s32[16,1,1]{2,1,0:T(1,128)S(1)}, u32[]{:S(2)}, u32[]{:S(2)}) async-start(s32[16,1,1]{2,1,0:T(1,128)} %broadcast_in_dim.9), calls=%async_computation | async-start | bytes 16384 | tf_op jit(solution)/shard_map/all_to_all | solution.py:126
  18.2 6.4 %all-to-all-done = s32[16,1,1]{2,1,0:T(1,128)S(1)} async-done(((s32[16,1,1]{2,1,0:T(1,128)}), s32[16,1,1]{2,1,0:T(1,128)S(1)}, u32[]{:S(2)}, u32[]{:S(2)}) %all-to-all-start) | async-done | bytes 96 | tf_op jit(solution)/shard_map/all_to_all | solution.py:126
  24.6 0.4 reduce
  24.9 0.5 and_select_fusion
  25.5 10.8 %shard_map.69 = f32[16,128,128]{2,1,0:T(8,128)} custom-call(s32[16]{0:T(128)} %get-tuple-element.7.rows_ref, s32[16]{0:T(128)} %get-tuple-element.6.cols_ref, bf16[256,8192]{1,0:T(8,128)(2,1)} %x_ref.1, bf16[256,1024]{1,0:T(8,128)(2,1)} %gv_ref.1), custom_call_target="tpu_custom_call" | custom-call | tf_op jit(solution)/shard_map/pallas_call | solution.py:96
  36.3 1.1 dynamic-slice_bitcast_fusion
  37.4 0.1 collective-permute-start
  37.5 1.9 %collective-permute-done = f32[8,128,128]{2,1,0:T(8,128)S(1)} collective-permute-done((f32[8,128,128]{2,1,0:T(8,128)S(1)}, f32[8,128,128]{2,1,0:T(8,128)S(1)}, u32[]{:S(2)}, u32[]{:S(2)}) %collective-permute-start) | collective-permute-done | bytes 524320 | tf_op jit(solution)/shard_map/ppermute | solution.py:135
  39.3 1.1 bitcast_add_fusion
  40.5 0.7 collective-permute-start.1
  41.1 14.0 %collective-permute-done.1 = f32[4,128,128]{2,1,0:T(8,128)S(1)} collective-permute-done((f32[4,128,128]{2,1,0:T(8,128)S(1)}, f32[4,128,128]{2,1,0:T(8,128)S(1)}, u32[]{:S(2)}, u32[]{:S(2)}) %collective-permute-start.1) | collective-permute-done | bytes 262176 | tf_op jit(solution)/shard_map/ppermute | solution.py:141
  55.1 0.7 bitcast_add_fusion.1
  55.8 54.1 %all-gather.3.cloned.1.call-done = bf16[8448,1024]{1,0:T(8,128)(2,1)} async-done(((bf16[528,1024]{1,0:T(8,128)(2,1)}), bf16[8448,1024]{1,0:T(8,128)(2,1)}) %all-gather.3.cloned.1.call-update) | async-done | bytes 17301520 | tf_op jit(solution)/shard_map/all_gather | solution.py:124
  109.9 4.7 %all-to-all-start.1 = ((f32[4,128,128]{2,1,0:T(8,128)}), f32[4,128,128]{2,1,0:T(8,128)S(1)}, u32[]{:S(2)}, u32[]{:S(2)}) async-start(f32[4,128,128]{2,1,0:T(8,128)} %bitcast_add_fusion.1), calls=%async_computation.1 | async-start | bytes 524288 | tf_op jit(solution)/shard_map/all_to_all | solution.py:146
  114.6 11.8 %shard_map.70 = bf16[256,8192]{1,0:T(8,128)(2,1)} custom-call(s32[16]{0:T(128)} %get-tuple-element.7.rows_ref, s32[16]{0:T(128)} %get-tuple-element.6.cols_ref, bf16[256,1024]{1,0:T(8,128)(2,1)} %gv_ref.1, bf16[16,528,1024]{2,1,0:T(8,128)(2,1)} %bitcast.15, bf16[16,528,1024]{2,1,0:T(8,128)(2,1)} %bitcast.16), custom_call_target="tpu_custom_call" | custom-call | tf_op jit(solution)/shard_map/pallas_call | solution.py:54
  126.5 0.0 all-to-all-done.1
  126.5 0.6 multiply_bitcast_fusion
  (2 shorter events, 0.0 us)
Async XLA Ops:
  7.2 102.7 %all-gather.3.cloned.1.call-start = ((), (), s32[]{:S(2)}) async-start(), calls=%async_computation.2 | async-start | bytes 18382848 | tf_op jit(solution)/shard_map/all_gather | solution.py:124
  10.8 13.8 %all-to-all-start = ((s32[16,1,1]{2,1,0:T(1,128)}), s32[16,1,1]{2,1,0:T(1,128)S(1)}, u32[]{:S(2)}, u32[]{:S(2)}) async-start(s32[16,1,1]{2,1,0:T(1,128)} %broadcast_in_dim.9), calls=%async_computation | async-start | bytes 16384 | tf_op jit(solution)/shard_map/all_to_all | solution.py:126
  37.4 2.0 %collective-permute-start = (f32[8,128,128]{2,1,0:T(8,128)S(1)}, f32[8,128,128]{2,1,0:T(8,128)S(1)}, u32[]{:S(2)}, u32[]{:S(2)}) collective-permute-start(f32[8,128,128]{2,1,0:T(8,128)S(1)} %dynamic-slice_bitcast_fusion), channel_id=1, source_target_pairs={{0,1},{1,0},{2,3},{3,2},{4,5},{5,4},{6,7},{7,6},{8,9},{9,8},{10,11... | collective-permute-start | bytes 1572872 | tf_op jit(solution)/shard_map/ppermute | solution.py:135
  40.5 14.6 %collective-permute-start.1 = (f32[4,128,128]{2,1,0:T(8,128)S(1)}, f32[4,128,128]{2,1,0:T(8,128)S(1)}, u32[]{:S(2)}, u32[]{:S(2)}) collective-permute-start(f32[4,128,128]{2,1,0:T(8,128)S(1)} %dynamic-slice_bitcast_fusion.1), channel_id=1, source_target_pairs={{0,2},{2,0},{1,3},{3,1},{4,6},{6,4},{5,7},{7,5},{8,10},{10,8},{9,1... | collective-permute-start | bytes 786440 | tf_op jit(solution)/shard_map/ppermute | solution.py:141
  109.9 16.6 %all-to-all-start.1 = ((f32[4,128,128]{2,1,0:T(8,128)}), f32[4,128,128]{2,1,0:T(8,128)S(1)}, u32[]{:S(2)}, u32[]{:S(2)}) async-start(f32[4,128,128]{2,1,0:T(8,128)} %bitcast_add_fusion.1), calls=%async_computation.1 | async-start | bytes 524288 | tf_op jit(solution)/shard_map/all_to_all | solution.py:146
Sparse Core Ops, SparseCore 0:
  10.1 99.7 all-gather.2

commit v13 on v11

--- a/solution.py
+++ b/solution.py
@@ -72,15 +72,33 @@
     rows, kv = base_weight.shape
     col_tiles = kv // TILE
     sub = TILE * TILE // kv
+    total = rows + sub
+    steps = 3 if total % 3 == 0 and (total // 3) % sub == 0 and total // 3 >= sub else 1
+    block = total // steps
+    last = rows - (steps - 1) * block
 
     def kernel(b_ref, d_ref, o_ref):
-        o_ref[:rows, :] = b_ref[...]
-        for a in range(col_tiles):
-            o_ref[rows:, a * TILE:(a + 1) * TILE] = d_ref[0, a * sub:(a + 1) * sub, :]
+        i = pl.program_id(0)
+
+        @pl.when(i < steps - 1)
+        def _():
+            o_ref[...] = b_ref[...]
+
+        @pl.when(i == steps - 1)
+        def _():
+            o_ref[:last, :] = b_ref[:last, :]
+            for a in range(col_tiles):
+                o_ref[last:, a * TILE:(a + 1) * TILE] = d_ref[0, a * sub:(a + 1) * sub, :]
 
     return pl.pallas_call(
         kernel,
-        out_shape=jax.ShapeDtypeStruct((rows + sub, kv), base_weight.dtype),
+        grid=(steps,),
+        in_specs=[
+            pl.BlockSpec((block, kv), lambda i: (i, 0)),
+            pl.BlockSpec((1, TILE, TILE), lambda i: (0, 0, 0)),
+        ],
+        out_specs=pl.BlockSpec((block, kv), lambda i: (i, 0)),
+        out_shape=jax.ShapeDtypeStruct((total, kv), base_weight.dtype),
     )(base_weight, tile_delta)
 
 

time: 132 us -> 133 us (level)
  no operation moved by 1% of the time
where the time goes in v13:
time: 133 us; the launch traced here: 132 us
  waiting for transfers between devices  74.1 us (56%)
  Pallas kernels  25.6 us (19%)
  between operations  14.7 us (11%)
  starting transfers between devices  12.1 us (9%)
  other arithmetic  3.48 us (3%)
  local copies, waits for them, and re-layouts  1.77 us (1%)
    all_gather x1, waiting for transfers between devices, body(): gathered = lax.all_gather(packed, DP, axis=0, tiled=False)  62.4 us
    pallas_call x1, Pallas kernels, merged_matmul(): pl.pallas_call(kernel, grid_spec=pltpu.PrefetchScalarGridSpec(num_scalar_...  11.7 us
    pallas_call x1, Pallas kernels, tile_partials(): pl.pallas_call(kernel, grid_spec=pltpu.PrefetchScalarGridSpec(num_scalar_...  10.8 us
    all_to_all x1, starting transfers between devices, body(): lax.all_to_all(jnp.broadcast_to(tile_ids, (n,)), DP, 0, 0, tiled=True)  7.41 us
    all_to_all x1, waiting for transfers between devices, body(): lax.all_to_all(jnp.broadcast_to(tile_ids, (n,)), DP, 0, 0, tiled=True)  6.36 us
    all_to_all x1, starting transfers between devices, body(): from_chips = lax.all_to_all(chip_sum, 'chips', 0, 0, tiled=True)  4.57 us
    all_to_all x1, waiting for transfers between devices, body(): from_chips = lax.all_to_all(chip_sum, 'chips', 0, 0, tiled=True)  3.2 us
    pallas_call x1, Pallas kernels, packed_shard(): pl.pallas_call(kernel, grid=(steps,), in_specs=[pl.BlockSpec((block, kv),...  3.07 us
  transfers between devices with their start and end apart: 4, of which 4 were waited for; matrix products, arithmetic and copies ran while one was open for 3% of the time, Pallas kernels for 17%

profile of v13, /device:TPU:0, one launch (start us, length us, event | category | flops | bytes accessed | tf_op | source)
XLA Modules:
  0.0 131.8 jit_solution(17875968987780697608)
XLA Ops:
  7.2 0.0 all-gather.3.cloned.1.call-start
  7.2 3.1 %shard_map.68 = bf16[528,1024]{1,0:T(8,128)(2,1)} custom-call(bf16[512,1024]{1,0:T(8,128)(2,1)} %b_ref.1, bf16[1,128,128]{2,1,0:T(8,128)(2,1)} %d_ref.1), custom_call_target="tpu_custom_call" | custom-call | tf_op jit(solution)/shard_map/pallas_call | solution.py:93
  10.3 0.0 all-gather.3.cloned.1.call-update
  10.9 0.6 broadcast_in_dim.9
  11.6 7.4 %all-to-all-start = ((s32[16,1,1]{2,1,0:T(1,128)}), s32[16,1,1]{2,1,0:T(1,128)S(1)}, u32[]{:S(2)}, u32[]{:S(2)}) async-start(s32[16,1,1]{2,1,0:T(1,128)} %broadcast_in_dim.9), calls=%async_computation | async-start | bytes 16384 | tf_op jit(solution)/shard_map/all_to_all | solution.py:142
  19.0 6.4 %all-to-all-done = s32[16,1,1]{2,1,0:T(1,128)S(1)} async-done(((s32[16,1,1]{2,1,0:T(1,128)}), s32[16,1,1]{2,1,0:T(1,128)S(1)}, u32[]{:S(2)}, u32[]{:S(2)}) %all-to-all-start) | async-done | bytes 96 | tf_op jit(solution)/shard_map/all_to_all | solution.py:142
  25.3 0.4 reduce
  25.7 0.5 and_select_fusion
  26.3 10.8 %shard_map.69 = f32[16,128,128]{2,1,0:T(8,128)} custom-call(s32[16]{0:T(128)} %get-tuple-element.7.rows_ref, s32[16]{0:T(128)} %get-tuple-element.6.cols_ref, bf16[256,8192]{1,0:T(8,128)(2,1)} %x_ref.1, bf16[256,1024]{1,0:T(8,128)(2,1)} %gv_ref.1), custom_call_target="tpu_custom_call" | custom-call | tf_op jit(solution)/shard_map/pallas_call | solution.py:114
  37.1 1.2 dynamic-slice_bitcast_fusion
  38.3 0.1 collective-permute-start
  38.3 2.2 %collective-permute-done = f32[8,128,128]{2,1,0:T(8,128)S(1)} collective-permute-done((f32[8,128,128]{2,1,0:T(8,128)S(1)}, f32[8,128,128]{2,1,0:T(8,128)S(1)}, u32[]{:S(2)}, u32[]{:S(2)}) %collective-permute-start) | collective-permute-done | bytes 524320 | tf_op jit(solution)/shard_map/ppermute | solution.py:151
  40.5 1.9 %bitcast_add_fusion = f32[8,128,128]{2,1,0:T(8,128)} fusion(f32[8,128,128]{2,1,0:T(8,128)S(1)} %collective-permute-done, f32[8,2,128,128]{3,2,1,0:T(8,128)} %bitcast.13, s32[]{:T(128)S(6)} %select_n.21), kind=kLoop, calls=%fused_computation | loop fusion | flops 131072 | bytes 1572868 | tf_op jit(solution)/shard_map/add | solution.py:151
  42.4 62.4 %all-gather.3.cloned.1.call-done = bf16[8448,1024]{1,0:T(8,128)(2,1)} async-done(((bf16[528,1024]{1,0:T(8,128)(2,1)}), bf16[8448,1024]{1,0:T(8,128)(2,1)}) %all-gather.3.cloned.1.call-update) | async-done | bytes 17301520 | tf_op jit(solution)/shard_map/all_gather | solution.py:140
  104.8 4.6 %all-to-all-start.1 = ((f32[8,128,128]{2,1,0:T(8,128)}), f32[8,128,128]{2,1,0:T(8,128)S(1)}, u32[]{:S(2)}, u32[]{:S(2)}) async-start(f32[8,128,128]{2,1,0:T(8,128)} %bitcast_add_fusion), calls=%async_computation.1 | async-start | bytes 1048576 | tf_op jit(solution)/shard_map/all_to_all | solution.py:153
  109.4 11.7 %shard_map.70 = bf16[256,8192]{1,0:T(8,128)(2,1)} custom-call(s32[16]{0:T(128)} %get-tuple-element.7.rows_ref, s32[16]{0:T(128)} %get-tuple-element.6.cols_ref, bf16[256,1024]{1,0:T(8,128)(2,1)} %gv_ref.1, bf16[16,528,1024]{2,1,0:T(8,128)(2,1)} %bitcast.10, bf16[16,528,1024]{2,1,0:T(8,128)(2,1)} %bitcast.11), custom_call_target="tpu_custom_call" | custom-call | tf_op jit(solution)/shard_map/pallas_call | solution.py:54
  121.1 3.2 %all-to-all-done.1 = f32[8,128,128]{2,1,0:T(8,128)S(1)} async-done(((f32[8,128,128]{2,1,0:T(8,128)}), f32[8,128,128]{2,1,0:T(8,128)S(1)}, u32[]{:S(2)}, u32[]{:S(2)}) %all-to-all-start.1) | async-done | bytes 524320 | tf_op jit(solution)/shard_map/all_to_all | solution.py:153
  124.3 0.6 multiply_bitcast_fusion
  (1 shorter events, 0.0 us)
Async XLA Ops:
  7.2 97.6 %all-gather.3.cloned.1.call-start = ((), (), s32[]{:S(2)}) async-start(), calls=%async_computation.2 | async-start | bytes 18382848 | tf_op jit(solution)/shard_map/all_gather | solution.py:140
  11.6 13.8 %all-to-all-start = ((s32[16,1,1]{2,1,0:T(1,128)}), s32[16,1,1]{2,1,0:T(1,128)S(1)}, u32[]{:S(2)}, u32[]{:S(2)}) async-start(s32[16,1,1]{2,1,0:T(1,128)} %broadcast_in_dim.9), calls=%async_computation | async-start | bytes 16384 | tf_op jit(solution)/shard_map/all_to_all | solution.py:142
  38.3 2.3 %collective-permute-start = (f32[8,128,128]{2,1,0:T(8,128)S(1)}, f32[8,128,128]{2,1,0:T(8,128)S(1)}, u32[]{:S(2)}, u32[]{:S(2)}) collective-permute-start(f32[8,128,128]{2,1,0:T(8,128)S(1)} %dynamic-slice_bitcast_fusion), channel_id=1, source_target_pairs={{0,1},{1,0},{2,3},{3,2},{4,5},{5,4},{6,7},{7,6},{8,9},{9,8},{10,11... | collective-permute-start | bytes 1572872 | tf_op jit(solution)/shard_map/ppermute | solution.py:151
  104.8 19.5 %all-to-all-start.1 = ((f32[8,128,128]{2,1,0:T(8,128)}), f32[8,128,128]{2,1,0:T(8,128)S(1)}, u32[]{:S(2)}, u32[]{:S(2)}) async-start(f32[8,128,128]{2,1,0:T(8,128)} %bitcast_add_fusion), calls=%async_computation.1 | async-start | bytes 1048576 | tf_op jit(solution)/shard_map/all_to_all | solution.py:153
Sparse Core Ops, SparseCore 0:
  10.4 94.3 all-gather.2

commit v14 on v11

--- a/solution.py
+++ b/solution.py
@@ -132,9 +132,10 @@
     other = lax.dynamic_index_in_dim(partial, 1 - core, axis=1, keepdims=False)
     chip_sum = mine + lax.ppermute(other, "core", [(0, 1), (1, 0)])
     gathered, chip_sum = lax.optimization_barrier((gathered, chip_sum))
-    from_chips = lax.all_to_all(chip_sum, "chips", 0, 0, tiled=True)
+    flat = chip_sum.reshape(chips, TILE * TILE)
+    from_chips = lax.all_to_all(flat, "chips", 0, 0, tiled=True)
     factor = 1.0 / math.sqrt(tokens_here * n)
-    grad_tiles = jnp.sum(from_chips, axis=0, keepdims=True) * factor
+    grad_tiles = jnp.sum(from_chips, axis=0).reshape(1, TILE, TILE) * factor
 
     grad_input = merged_matmul(tile_rows, tile_cols, grad_values, gathered, shard)
     return (grad_input, grad_tiles)

time: 132 us -> 133 us (level)
  no operation moved by 1% of the time
where the time goes in v14:
time: 133 us; the launch traced here: 132 us
  waiting for transfers between devices  74.7 us (56%)
  Pallas kernels  24.8 us (19%)
  between operations  14.7 us (11%)
  starting transfers between devices  12.1 us (9%)
  other arithmetic  3.83 us (3%)
  local copies, waits for them, and re-layouts  1.68 us (1%)
    all_gather x1, waiting for transfers between devices, body(): gathered = lax.all_gather(packed, DP, axis=0, tiled=False)  63.3 us
    pallas_call x1, Pallas kernels, merged_matmul(): pl.pallas_call(kernel, grid_spec=pltpu.PrefetchScalarGridSpec(num_scalar_...  11.7 us
    pallas_call x1, Pallas kernels, tile_partials(): pl.pallas_call(kernel, grid_spec=pltpu.PrefetchScalarGridSpec(num_scalar_...  10.8 us
    all_to_all x1, starting transfers between devices, body(): lax.all_to_all(jnp.broadcast_to(tile_ids, (n,)), DP, 0, 0, tiled=True)  7.41 us
    all_to_all x1, waiting for transfers between devices, body(): lax.all_to_all(jnp.broadcast_to(tile_ids, (n,)), DP, 0, 0, tiled=True)  6.36 us
    all_to_all x1, starting transfers between devices, body(): from_chips = lax.all_to_all(flat, 'chips', 0, 0, tiled=True)  4.53 us
    all_to_all x1, waiting for transfers between devices, body(): from_chips = lax.all_to_all(flat, 'chips', 0, 0, tiled=True)  3.2 us
  transfers between devices with their start and end apart: 4, of which 4 were waited for; matrix products, arithmetic and copies ran while one was open for 3% of the time, Pallas kernels for 17%

profile of v14, /device:TPU:0, one launch (start us, length us, event | category | flops | bytes accessed | tf_op | source)
XLA Modules:
  0.0 131.8 jit_solution(5086038912002252234)
XLA Ops:
  7.2 0.0 all-gather.3.cloned.1.call-start
  7.2 2.3 %shard_map.68 = bf16[528,1024]{1,0:T(8,128)(2,1)} custom-call(bf16[512,1024]{1,0:T(8,128)(2,1)} %b_ref.1, bf16[1,128,128]{2,1,0:T(8,128)(2,1)} %d_ref.1), custom_call_target="tpu_custom_call" | custom-call | tf_op jit(solution)/shard_map/pallas_call | solution.py:81
  9.5 0.0 all-gather.3.cloned.1.call-update
  10.2 0.6 broadcast_in_dim.8
  10.8 7.4 %all-to-all-start = ((s32[16,1,1]{2,1,0:T(1,128)}), s32[16,1,1]{2,1,0:T(1,128)S(1)}, u32[]{:S(2)}, u32[]{:S(2)}) async-start(s32[16,1,1]{2,1,0:T(1,128)} %broadcast_in_dim.8), calls=%async_computation | async-start | bytes 16384 | tf_op jit(solution)/shard_map/all_to_all | solution.py:124
  18.2 6.4 %all-to-all-done = s32[16,1,1]{2,1,0:T(1,128)S(1)} async-done(((s32[16,1,1]{2,1,0:T(1,128)}), s32[16,1,1]{2,1,0:T(1,128)S(1)}, u32[]{:S(2)}, u32[]{:S(2)}) %all-to-all-start) | async-done | bytes 96 | tf_op jit(solution)/shard_map/all_to_all | solution.py:124
  24.6 0.4 reduce.1
  24.9 0.5 and_select_fusion
  25.5 10.8 %shard_map.69 = f32[16,128,128]{2,1,0:T(8,128)} custom-call(s32[16]{0:T(128)} %get-tuple-element.7.rows_ref, s32[16]{0:T(128)} %get-tuple-element.6.cols_ref, bf16[256,8192]{1,0:T(8,128)(2,1)} %x_ref.1, bf16[256,1024]{1,0:T(8,128)(2,1)} %gv_ref.1), custom_call_target="tpu_custom_call" | custom-call | tf_op jit(solution)/shard_map/pallas_call | solution.py:96
  36.3 1.1 dynamic-slice_bitcast_fusion
  37.4 0.1 collective-permute-start
  37.5 1.9 %collective-permute-done = f32[8,128,128]{2,1,0:T(8,128)S(1)} collective-permute-done((f32[8,128,128]{2,1,0:T(8,128)S(1)}, f32[8,128,128]{2,1,0:T(8,128)S(1)}, u32[]{:S(2)}, u32[]{:S(2)}) %collective-permute-start) | collective-permute-done | bytes 524320 | tf_op jit(solution)/shard_map/ppermute | solution.py:133
  39.4 1.9 %bitcast_add_fusion = f32[8,128,128]{2,1,0:T(8,128)} fusion(f32[8,128,128]{2,1,0:T(8,128)S(1)} %collective-permute-done, f32[8,2,128,128]{3,2,1,0:T(8,128)} %bitcast.14, s32[]{:T(128)S(6)} %select_n.21), kind=kLoop, calls=%fused_computation | loop fusion | flops 131072 | bytes 1572868 | tf_op jit(solution)/shard_map/add | solution.py:133
  41.2 63.3 %all-gather.3.cloned.1.call-done = bf16[8448,1024]{1,0:T(8,128)(2,1)} async-done(((bf16[528,1024]{1,0:T(8,128)(2,1)}), bf16[8448,1024]{1,0:T(8,128)(2,1)}) %all-gather.3.cloned.1.call-update) | async-done | bytes 17301520 | tf_op jit(solution)/shard_map/all_gather | solution.py:122
  104.5 4.5 %all-to-all-start.1 = ((f32[8,1,16384]{2,1,0:T(1,128)}), f32[8,1,16384]{2,1,0:T(1,128)S(1)}, u32[]{:S(2)}, u32[]{:S(2)}) async-start(f32[8,1,16384]{2,1,0:T(1,128)} %bitcast.5), calls=%async_computation.1 | async-start | bytes 1048576 | tf_op jit(solution)/shard_map/all_to_all | solution.py:136
  109.0 11.7 %shard_map.70 = bf16[256,8192]{1,0:T(8,128)(2,1)} custom-call(s32[16]{0:T(128)} %get-tuple-element.7.rows_ref, s32[16]{0:T(128)} %get-tuple-element.6.cols_ref, bf16[256,1024]{1,0:T(8,128)(2,1)} %gv_ref.1, bf16[16,528,1024]{2,1,0:T(8,128)(2,1)} %bitcast.11, bf16[16,528,1024]{2,1,0:T(8,128)(2,1)} %bitcast.12), custom_call_target="tpu_custom_call" | custom-call | tf_op jit(solution)/shard_map/pallas_call | solution.py:54
  120.7 3.2 %all-to-all-done.1 = f32[8,1,16384]{2,1,0:T(1,128)S(1)} async-done(((f32[8,1,16384]{2,1,0:T(1,128)}), f32[8,1,16384]{2,1,0:T(1,128)S(1)}, u32[]{:S(2)}, u32[]{:S(2)}) %all-to-all-start.1) | async-done | bytes 524320 | tf_op jit(solution)/shard_map/all_to_all | solution.py:136
  123.9 0.4 reduce_sum.9
  124.3 0.6 multiply_bitcast_fusion
Async XLA Ops:
  7.2 97.3 %all-gather.3.cloned.1.call-start = ((), (), s32[]{:S(2)}) async-start(), calls=%async_computation.2 | async-start | bytes 18382848 | tf_op jit(solution)/shard_map/all_gather | solution.py:122
  10.8 13.8 %all-to-all-start = ((s32[16,1,1]{2,1,0:T(1,128)}), s32[16,1,1]{2,1,0:T(1,128)S(1)}, u32[]{:S(2)}, u32[]{:S(2)}) async-start(s32[16,1,1]{2,1,0:T(1,128)} %broadcast_in_dim.8), calls=%async_computation | async-start | bytes 16384 | tf_op jit(solution)/shard_map/all_to_all | solution.py:124
  37.4 2.0 %collective-permute-start = (f32[8,128,128]{2,1,0:T(8,128)S(1)}, f32[8,128,128]{2,1,0:T(8,128)S(1)}, u32[]{:S(2)}, u32[]{:S(2)}) collective-permute-start(f32[8,128,128]{2,1,0:T(8,128)S(1)} %dynamic-slice_bitcast_fusion), channel_id=1, source_target_pairs={{0,1},{1,0},{2,3},{3,2},{4,5},{5,4},{6,7},{7,6},{8,9},{9,8},{10,11... | collective-permute-start | bytes 1572872 | tf_op jit(solution)/shard_map/ppermute | solution.py:133
  104.5 19.4 %all-to-all-start.1 = ((f32[8,1,16384]{2,1,0:T(1,128)}), f32[8,1,16384]{2,1,0:T(1,128)S(1)}, u32[]{:S(2)}, u32[]{:S(2)}) async-start(f32[8,1,16384]{2,1,0:T(1,128)} %bitcast.5), calls=%async_computation.1 | async-start | bytes 1048576 | tf_op jit(solution)/shard_map/all_to_all | solution.py:136
Sparse Core Ops, SparseCore 0:
  10.1 94.3 all-gather.2
